TPU v7x, 512 devices: a whole 4x4x16 slice. The times are simulated.
512 devices in a mesh: path: 32 (over x, y, core), tensor: 16 (over z).
Axes of the slice: x: 4, y: 4, z: 16, core: 2. Of those that a mesh axis runs over, the one named last changes fastest.
Arguments:
- hidden_in: bfloat16 [12288, 2048], P(('path', 'tensor')), may hold values from -120 to 120
- teacher: bfloat16 [12288, 2048], P('path'), may hold values from -3 to 3
- params: bfloat16 [3, 3, 7168, 2048], P(None, None, ('tensor', 'path')), may hold values from -4 to 4
- momentum: float32 [3, 3, 7168, 2048], P(None, None, ('tensor', 'path')), may hold values from -3 to 3
- path_alive: int32 [32], replicated, may hold values from 0 to 1, as said below
- path_module: int32 [32], replicated, may hold values from 0 to 2, as said below
Outputs:
- new_params: bfloat16 [3, 3, 7168, 2048], P(None, None, ('tensor', 'path'))
- new_momentum: float32 [3, 3, 7168, 2048], P(None, None, ('tensor', 'path'))
Inputs may be any that keep to these rules, and one draw needn't show every extreme that they name: `path_alive`: at least one path is dead. `path_module`: every one of the 3 modules is used by at least one path whose path_alive entry is 1.
All inputs are finite; a program needn't handle non-finite values.
Results may differ from a plain program's by a relative error of at most 0.0047.
Values may be sent and summed in bfloat16 or wider, within the bound.
No kernel may reach another device: no remote copies, remote signals or barrier semaphores. Data moves between devices by JAX's collectives and lax.ppermute only.
A program may use at most 64 MiB of HBM per device.

v0:
```python
import math

import jax
import jax.numpy as jnp
from jax import lax
from jax.sharding import PartitionSpec as P

D = 2048
FW = 7168


def module_sums(weighting, received):
    flat = received.reshape(received.shape[0], -1)
    return lax.dot_general(
        weighting, flat, (((0,), (0,)), ((), ())), preferred_element_type=jnp.float32
    )


def per_device(hidden_in, teacher, params, momentum, path_alive, path_module):
    module_count = params.shape[0]
    block_rows = params.shape[2]
    width = params.shape[3]
    path_count = path_alive.shape[0]
    contract_last = (((1,), (1,)), ((), ()))
    contract_first = (((0,), (0,)), ((), ()))
    gate_pick = jnp.take(params[:, 0], path_module, axis=0)
    up_pick = jnp.take(params[:, 1], path_module, axis=0)
    down_pick = jnp.take(params[:, 2], path_module, axis=0)
    gate_rows, up_rows, down_rows = (
        lax.all_to_all(gate_pick, "path", split_axis=0, concat_axis=0, tiled=True),
        lax.all_to_all(up_pick, "path", split_axis=0, concat_axis=0, tiled=True),
        lax.all_to_all(down_pick, "path", split_axis=0, concat_axis=0, tiled=True),
    )
    local_rows = path_count * block_rows
    gate_rows = gate_rows.reshape(local_rows, width)
    up_rows = up_rows.reshape(local_rows, width)
    down_rows = down_rows.reshape(local_rows, width)
    rows_in = lax.all_gather(hidden_in, "tensor", axis=0, tiled=True)
    mean_sq = jnp.mean(jnp.square(rows_in.astype(jnp.float32)), axis=1, keepdims=True)
    normed = (rows_in.astype(jnp.float32) * lax.rsqrt(mean_sq + 1e-05)).astype(jnp.bfloat16)
    gate_pre = lax.dot_general(
        normed, gate_rows, contract_last, preferred_element_type=jnp.float32
    ) / math.sqrt(D)
    up_proj = lax.dot_general(
        normed, up_rows, contract_last, preferred_element_type=jnp.float32
    ) / math.sqrt(D)
    sigmoid_gate = jax.nn.sigmoid(gate_pre)
    activated = gate_pre * sigmoid_gate
    hidden = (activated * up_proj).astype(jnp.bfloat16)
    partial_out = jnp.dot(hidden, down_rows, preferred_element_type=jnp.float32) / math.sqrt(FW)
    output = lax.psum(partial_out, "tensor")
    cotangent = (4.0 * (output - teacher.astype(jnp.float32))).astype(jnp.bfloat16)
    down_delta = (
        lax.dot_general(hidden, cotangent, contract_first, preferred_element_type=jnp.float32)
        / math.sqrt(FW)
    ).astype(jnp.bfloat16)
    hidden_grad = lax.dot_general(
        cotangent, down_rows, contract_last, preferred_element_type=jnp.float32
    ) / math.sqrt(FW)
    gate_grad = (
        hidden_grad * up_proj * sigmoid_gate * (1.0 + gate_pre * (1.0 - sigmoid_gate))
    ).astype(jnp.bfloat16)
    up_grad = (hidden_grad * activated).astype(jnp.bfloat16)
    member = (path_module[:, None] == jnp.arange(module_count, dtype=jnp.int32)[None, :]).astype(
        jnp.int32
    ) * path_alive[:, None]
    weighting = member.astype(jnp.bfloat16)
    counts = jnp.sum(member, axis=0).astype(jnp.float32)
    piece_shape = (path_count, block_rows, width)
    gate_delta = (
        lax.dot_general(gate_grad, normed, contract_first, preferred_element_type=jnp.float32)
        / math.sqrt(D)
    ).astype(jnp.bfloat16)
    up_delta = (
        lax.dot_general(up_grad, normed, contract_first, preferred_element_type=jnp.float32)
        / math.sqrt(D)
    ).astype(jnp.bfloat16)
    gate_got, up_got, down_got = (
        lax.all_to_all(
            gate_delta.reshape(piece_shape), "path", split_axis=0, concat_axis=0, tiled=True
        ),
        lax.all_to_all(
            up_delta.reshape(piece_shape), "path", split_axis=0, concat_axis=0, tiled=True
        ),
        lax.all_to_all(
            down_delta.reshape(piece_shape), "path", split_axis=0, concat_axis=0, tiled=True
        ),
    )
    summed = jnp.stack(
        [
            module_sums(weighting, gate_got),
            module_sums(weighting, up_got),
            module_sums(weighting, down_got),
        ],
        axis=1,
    )
    summed = summed.reshape(module_count, 3, block_rows, width)
    mean_delta = summed / counts[:, None, None, None]
    new_momentum = 0.9 * momentum + mean_delta
    new_params = (params.astype(jnp.float32) - 0.7 * (mean_delta + 0.9 * new_momentum)).astype(
        jnp.bfloat16
    )
    return (new_params, new_momentum)


def solution(mesh):
    return jax.shard_map(
        per_device,
        mesh=mesh,
        in_specs=(
            P(("path", "tensor"), None),
            P("path", None),
            P(None, None, ("tensor", "path"), None),
            P(None, None, ("tensor", "path"), None),
            P(),
            P(),
        ),
        out_specs=(
            P(None, None, ("tensor", "path"), None),
            P(None, None, ("tensor", "path"), None),
        ),
        check_vma=False,
    )
```

profile of v0, /device:TPU:1, one launch (start us, length us, event | category | flops | bytes accessed | tf_op | source)
XLA Modules:
  0.0 420.3 jit_solution(7197902476013149992)
XLA Ops:
  10.3 2.0 gather_fusion.1
  12.4 2.0 gather_fusion.2
  14.4 4.8 %broadcast_select_fusion = (bf16[32,14,2048]{2,1,0:T(8,128)(2,1)}, bf16[32,14,2048]{2,1,0:T(8,128)(2,1)}, bf16[32,14,2048]{2,1,0:T(8,128)(2,1)S(1)}) fusion(bf16[32,14,2048]{2,1,0:T(8,128)(2,1)} %gather_fusion.2, pred[32]{0:T(512)(128)(4,1)S(1)} %compare_and_fusion, bf16[32,14,2048]{2,1,0:T(8,128)(2,1)} %gather_fusion.1, bf16[32,14,2048]{2,1,0:T(8,128)(2,1)S(1)} %gather_fusion), kind=kLoop, calls=%fused_computation.15 | loop fusion | flops 2752512 | bytes 11010080 | tf_op jit(solution)/shard_map/jit(_take)/select_n | solution.py:28
  19.2 37.7 %all_to_all.30 = bf16[32,14,2048]{2,1,0:T(8,128)(2,1)S(1)} all-to-all(bf16[32,14,2048]{2,1,0:T(8,128)(2,1)S(1)} %get-tuple-element.14), channel_id=1, replica_groups=mesh['path'=32,'tensor'=16] {'path'}, dimensions={0} | all-to-all | bytes 3670016 | tf_op jit(solution)/shard_map/all_to_all | solution.py:30
  56.9 4.5 %all-to-all-start.1 = ((bf16[32,14,2048]{2,1,0:T(8,128)(2,1)}), bf16[32,14,2048]{2,1,0:T(8,128)(2,1)}, u32[]{:S(2)}, u32[]{:S(2)}) async-start(bf16[32,14,2048]{2,1,0:T(8,128)(2,1)} %get-tuple-element.13), calls=%async_computation.1 | async-start | bytes 4194304 | tf_op jit(solution)/shard_map/all_to_all | solution.py:31
  62.2 27.6 %all-to-all-done.1 = bf16[32,14,2048]{2,1,0:T(8,128)(2,1)} async-done(((bf16[32,14,2048]{2,1,0:T(8,128)(2,1)}), bf16[32,14,2048]{2,1,0:T(8,128)(2,1)}, u32[]{:S(2)}, u32[]{:S(2)}) %all-to-all-start.1) | async-done | bytes 1835040 | tf_op jit(solution)/shard_map/all_to_all | solution.py:31
  89.9 5.2 %all-to-all-start.2 = ((bf16[32,14,2048]{2,1,0:T(8,128)(2,1)}), bf16[32,14,2048]{2,1,0:T(8,128)(2,1)}, u32[]{:S(2)}, u32[]{:S(2)}) async-start(bf16[32,14,2048]{2,1,0:T(8,128)(2,1)} %get-tuple-element.12), calls=%async_computation.2 | async-start | bytes 4194304 | tf_op jit(solution)/shard_map/all_to_all | solution.py:32
  96.6 3.7 reshape.75
  100.3 23.2 %all-to-all-done.2 = bf16[32,14,2048]{2,1,0:T(8,128)(2,1)} async-done(((bf16[32,14,2048]{2,1,0:T(8,128)(2,1)}), bf16[32,14,2048]{2,1,0:T(8,128)(2,1)}, u32[]{:S(2)}, u32[]{:S(2)}) %all-to-all-start.2) | async-done | bytes 1835040 | tf_op jit(solution)/shard_map/all_to_all | solution.py:32
  123.5 2.5 reshape.76
  126.1 4.1 all-gather.2.cloned.1.call-done
  130.2 1.8 fusion
  132.0 3.3 convolution_multiply_fusion.3
  135.4 2.1 multiply_convert_fusion.6
  138.2 2.7 convolution_multiply_fusion
  140.9 147.1 %all-reduce.2.cloned.1.call-done = f32[384,2048]{1,0:T(8,128)} async-done(((f32[384,2048]{1,0:T(8,128)}), f32[384,2048]{1,0:T(8,128)}) %all-reduce.2.cloned.1.call-update) | async-done | bytes 3145744 | tf_op jit(solution)/shard_map/psum | solution.py:51
  288.0 3.2 convolution_multiply_fusion.1
  295.1 16.8 %all-to-all-start.3 = ((bf16[32,14,2048]{2,1,0:T(8,128)(2,1)}), bf16[32,14,2048]{2,1,0:T(8,128)(2,1)}, u32[]{:S(2)}, u32[]{:S(2)}) async-start(bf16[32,14,2048]{2,1,0:T(8,128)(2,1)} %reshape.77), calls=%async_computation.3 | async-start | bytes 4194304 | tf_op jit(solution)/shard_map/all_to_all | solution.py:79
  311.9 3.1 multiply_convert_fusion.1
  315.0 1.7 reshape.80
  316.7 23.6 %all-to-all-done.3 = bf16[32,14,2048]{2,1,0:T(8,128)(2,1)} async-done(((bf16[32,14,2048]{2,1,0:T(8,128)(2,1)}), bf16[32,14,2048]{2,1,0:T(8,128)(2,1)}, u32[]{:S(2)}, u32[]{:S(2)}) %all-to-all-start.3) | async-done | bytes 1835040 | tf_op jit(solution)/shard_map/all_to_all | solution.py:79
  340.3 5.2 %all-to-all-start.4 = ((bf16[32,14,2048]{2,1,0:T(8,128)(2,1)}), bf16[32,14,2048]{2,1,0:T(8,128)(2,1)}, u32[]{:S(2)}, u32[]{:S(2)}) async-start(bf16[32,14,2048]{2,1,0:T(8,128)(2,1)} %reshape.80), calls=%async_computation.4 | async-start | bytes 4194304 | tf_op jit(solution)/shard_map/all_to_all | solution.py:82
  345.5 3.2 multiply_convert_fusion
  348.7 1.6 reshape.83
  350.3 23.7 %all-to-all-done.4 = bf16[32,14,2048]{2,1,0:T(8,128)(2,1)} async-done(((bf16[32,14,2048]{2,1,0:T(8,128)(2,1)}), bf16[32,14,2048]{2,1,0:T(8,128)(2,1)}, u32[]{:S(2)}, u32[]{:S(2)}) %all-to-all-start.4) | async-done | bytes 1835040 | tf_op jit(solution)/shard_map/all_to_all | solution.py:82
  374.0 4.5 %all-to-all-start.5 = ((bf16[32,14,2048]{2,1,0:T(8,128)(2,1)}), bf16[32,14,2048]{2,1,0:T(8,128)(2,1)S(1)}, u32[]{:S(2)}, u32[]{:S(2)}) async-start(bf16[32,14,2048]{2,1,0:T(8,128)(2,1)} %reshape.83), calls=%async_computation.5 | async-start | bytes 4194304 | tf_op jit(solution)/shard_map/all_to_all | solution.py:85
  378.6 3.6 convolution_bitcast_fusion.2
  382.2 4.4 %convolution_bitcast_fusion.1 = f32[3,1,14,2048]{3,0,2,1:T(4,128)} fusion(s32[32]{0:T(128)S(1)} %copy-done.9, s32[32]{0:T(128)S(1)} %copy-done.10, bf16[4,8,14,2048]{3,2,1,0:T(8,128)(2,1)} %bitcast.18), kind=kOutput, calls=%fused_computation.13 | convolution fusion | flops 5505312 | bytes 2179328 | tf_op jit(solution)/shard_map/dot_general | solution.py:14
  386.6 20.2 %all-to-all-done.5 = bf16[32,14,2048]{2,1,0:T(8,128)(2,1)S(1)} async-done(((bf16[32,14,2048]{2,1,0:T(8,128)(2,1)}), bf16[32,14,2048]{2,1,0:T(8,128)(2,1)S(1)}, u32[]{:S(2)}, u32[]{:S(2)}) %all-to-all-start.5) | async-done | bytes 1835040 | tf_op jit(solution)/shard_map/all_to_all | solution.py:85
  406.9 2.0 convolution_bitcast_fusion
  408.9 1.7 fusion.8
  410.7 1.6 copy.18
  (44 shorter events, 11.5 us)
Async XLA Ops:
  56.9 32.9 %all-to-all-start.1 = ((bf16[32,14,2048]{2,1,0:T(8,128)(2,1)}), bf16[32,14,2048]{2,1,0:T(8,128)(2,1)}, u32[]{:S(2)}, u32[]{:S(2)}) async-start(bf16[32,14,2048]{2,1,0:T(8,128)(2,1)} %get-tuple-element.13), calls=%async_computation.1 | async-start | bytes 4194304 | tf_op jit(solution)/shard_map/all_to_all | solution.py:31
  61.5 68.7 %all-gather.2.cloned.1.call-start = ((), (), s32[]{:S(2)}) async-start(), calls=%async_computation.6 | async-start | bytes 1671168 | tf_op jit(solution)/shard_map/all_gather | solution.py:38
  89.9 33.7 %all-to-all-start.2 = ((bf16[32,14,2048]{2,1,0:T(8,128)(2,1)}), bf16[32,14,2048]{2,1,0:T(8,128)(2,1)}, u32[]{:S(2)}, u32[]{:S(2)}) async-start(bf16[32,14,2048]{2,1,0:T(8,128)(2,1)} %get-tuple-element.12), calls=%async_computation.2 | async-start | bytes 4194304 | tf_op jit(solution)/shard_map/all_to_all | solution.py:32
  95.0 193.0 %all-reduce.2.cloned.1.call-start = ((), (), s32[]{:S(2)}) async-start(), calls=%async_computation.7 | async-start | bytes 6291456 | tf_op jit(solution)/shard_map/psum | solution.py:51
  132.0 3.4 copy-start.3
  132.0 3.4 copy-start.4
  135.3 2.1 copy-start.11
  137.4 0.7 copy-start.1
  140.9 147.2 %copy-start = (bf16[384,2048]{1,0:T(8,128)(2,1)S(1)}, bf16[384,2048]{1,0:T(8,128)(2,1)}, u32[]{:S(2)}) copy-start(bf16[384,2048]{1,0:T(8,128)(2,1)} %param.9) | copy-start | bytes 4718596
  288.0 4.1 copy-start.5
  288.0 4.1 copy-start.12
  288.0 4.1 copy-start.13
  291.2 0.9 copy-start.7
  295.1 45.2 %all-to-all-start.3 = ((bf16[32,14,2048]{2,1,0:T(8,128)(2,1)}), bf16[32,14,2048]{2,1,0:T(8,128)(2,1)}, u32[]{:S(2)}, u32[]{:S(2)}) async-start(bf16[32,14,2048]{2,1,0:T(8,128)(2,1)} %reshape.77), calls=%async_computation.3 | async-start | bytes 4194304 | tf_op jit(solution)/shard_map/all_to_all | solution.py:79
  340.3 33.6 %all-to-all-start.4 = ((bf16[32,14,2048]{2,1,0:T(8,128)(2,1)}), bf16[32,14,2048]{2,1,0:T(8,128)(2,1)}, u32[]{:S(2)}, u32[]{:S(2)}) async-start(bf16[32,14,2048]{2,1,0:T(8,128)(2,1)} %reshape.80), calls=%async_computation.4 | async-start | bytes 4194304 | tf_op jit(solution)/shard_map/all_to_all | solution.py:82
  350.3 28.2 %copy-start.9 = (s32[32]{0:T(128)S(1)}, s32[32]{0:T(128)}, u32[]{:S(2)}) copy-start(s32[32]{0:T(128)} %param.12) | copy-start | bytes 388
  350.3 28.2 %copy-start.10 = (s32[32]{0:T(128)S(1)}, s32[32]{0:T(128)}, u32[]{:S(2)}) copy-start(s32[32]{0:T(128)} %param.13) | copy-start | bytes 388
  374.0 32.9 %all-to-all-start.5 = ((bf16[32,14,2048]{2,1,0:T(8,128)(2,1)}), bf16[32,14,2048]{2,1,0:T(8,128)(2,1)S(1)}, u32[]{:S(2)}, u32[]{:S(2)}) async-start(bf16[32,14,2048]{2,1,0:T(8,128)(2,1)} %reshape.83), calls=%async_computation.5 | async-start | bytes 4194304 | tf_op jit(solution)/shard_map/all_to_all | solution.py:85
  386.6 22.3 %copy-start.2 = (bf16[3,3,14,2048]{3,2,1,0:T(8,128)(2,1)S(1)}, bf16[3,3,14,2048]{3,2,1,0:T(8,128)(2,1)}, u32[]{:S(2)}) copy-start(bf16[3,3,14,2048]{3,2,1,0:T(8,128)(2,1)} %param.10) | copy-start | bytes 1548292
  406.9 2.1 copy-start.6
  406.9 2.1 copy-start.8
Sparse Core Ops, SparseCore 0:
  64.4 65.7 all-gather.1
  141.0 146.9 all-reduce.1
where the time goes:
time: 421 us; the launch traced here: 420 us
  waiting for transfers between devices  270 us (64%)
  blocking collectives  37.7 us (9%)
  starting transfers between devices  36.3 us (9%)
  matrix products  29 us (7%)
  local copies, waits for them, and re-layouts  23 us (5%)
  between operations  14.2 us (3%)
  other arithmetic  9.82 us (2%)
    psum x1, waiting for transfers between devices, per_device(): output = lax.psum(partial_out, 'tensor')  147 us
    all_to_all x1, blocking collectives, per_device(): lax.all_to_all(gate_pick, 'path', split_axis=0, concat_axis=0, tiled=True)  37.7 us
    all_to_all x1, waiting for transfers between devices, per_device(): lax.all_to_all(up_pick, 'path', split_axis=0, concat_axis=0, tiled=True)  27.6 us
    all_to_all x1, waiting for transfers between devices, per_device(): lax.all_to_all(up_delta.reshape(piece_shape), 'path', split_axis=0, conca...  23.7 us
    all_to_all x1, waiting for transfers between devices, per_device(): lax.all_to_all(gate_delta.reshape(piece_shape), 'path', split_axis=0, con...  23.6 us
    all_to_all x1, waiting for transfers between devices, per_device(): lax.all_to_all(down_pick, 'path', split_axis=0, concat_axis=0, tiled=True)  23.2 us
    all_to_all x1, waiting for transfers between devices, per_device(): lax.all_to_all(down_delta.reshape(piece_shape), 'path', split_axis=0, con...  20.2 us
    all_to_all x1, starting transfers between devices, per_device(): lax.all_to_all(gate_delta.reshape(piece_shape), 'path', split_axis=0, con...  16.8 us
  transfers between devices with their start and end apart: 7, of which 7 were waited for; matrix products, arithmetic and copies ran while one was open for 6% of the time, Pallas kernels for 0%

commit v1 on v0

v1 whole, which is shorter than its diff:
```python
import math

import jax
import jax.numpy as jnp
from jax import lax
from jax.sharding import PartitionSpec as P

D = 2048
FW = 7168


def per_device(hidden_in, teacher, params, momentum, path_alive, path_module):
    module_count = params.shape[0]
    block_rows = params.shape[2]
    width = params.shape[3]
    path_count = path_alive.shape[0]
    contract_last = (((1,), (1,)), ((), ()))
    contract_first = (((0,), (0,)), ((), ()))
    picked = jnp.take(params, path_module, axis=0)
    rows = lax.all_to_all(picked, "path", split_axis=0, concat_axis=0, tiled=True)
    local_rows = path_count * block_rows
    rows = jnp.moveaxis(rows, 1, 0).reshape(3, local_rows, width)
    gate_rows, up_rows, down_rows = rows[0], rows[1], rows[2]
    own = hidden_in.astype(jnp.float32)
    mean_sq = jnp.mean(jnp.square(own), axis=1, keepdims=True)
    own_normed = (own * lax.rsqrt(mean_sq + 1e-05)).astype(jnp.bfloat16)
    normed = lax.all_gather(own_normed, "tensor", axis=0, tiled=True)
    gate_pre = lax.dot_general(
        normed, gate_rows, contract_last, preferred_element_type=jnp.float32
    ) / math.sqrt(D)
    up_proj = lax.dot_general(
        normed, up_rows, contract_last, preferred_element_type=jnp.float32
    ) / math.sqrt(D)
    sigmoid_gate = jax.nn.sigmoid(gate_pre)
    activated = gate_pre * sigmoid_gate
    hidden = (activated * up_proj).astype(jnp.bfloat16)
    partial_out = jnp.dot(hidden, down_rows, preferred_element_type=jnp.float32) / math.sqrt(FW)
    out_rows = lax.psum_scatter(partial_out, "tensor", scatter_dimension=0, tiled=True)
    own_count = out_rows.shape[0]
    start = lax.axis_index("tensor") * own_count
    target = lax.dynamic_slice_in_dim(teacher, start, own_count, 0)
    own_cot = (4.0 * (out_rows - target.astype(jnp.float32))).astype(jnp.bfloat16)
    cotangent = lax.all_gather(own_cot, "tensor", axis=0, tiled=True)
    down_delta = (
        lax.dot_general(hidden, cotangent, contract_first, preferred_element_type=jnp.float32)
        / math.sqrt(FW)
    ).astype(jnp.bfloat16)
    hidden_grad = lax.dot_general(
        cotangent, down_rows, contract_last, preferred_element_type=jnp.float32
    ) / math.sqrt(FW)
    gate_grad = (
        hidden_grad * up_proj * sigmoid_gate * (1.0 + gate_pre * (1.0 - sigmoid_gate))
    ).astype(jnp.bfloat16)
    up_grad = (hidden_grad * activated).astype(jnp.bfloat16)
    gate_delta = (
        lax.dot_general(gate_grad, normed, contract_first, preferred_element_type=jnp.float32)
        / math.sqrt(D)
    ).astype(jnp.bfloat16)
    up_delta = (
        lax.dot_general(up_grad, normed, contract_first, preferred_element_type=jnp.float32)
        / math.sqrt(D)
    ).astype(jnp.bfloat16)
    member = (path_module[:, None] == jnp.arange(module_count, dtype=jnp.int32)[None, :]).astype(
        jnp.int32
    ) * path_alive[:, None]
    weighting = member.astype(jnp.bfloat16)
    counts = jnp.sum(member, axis=0).astype(jnp.float32)
    deltas = jnp.stack([gate_delta, up_delta, down_delta]).reshape(3, path_count, block_rows, width)
    got = lax.all_to_all(
        jnp.moveaxis(deltas, 1, 0), "path", split_axis=0, concat_axis=0, tiled=True
    )
    summed = lax.dot_general(
        weighting, got.reshape(path_count, -1), contract_first, preferred_element_type=jnp.float32
    )
    summed = summed.reshape(module_count, 3, block_rows, width)
    mean_delta = summed / counts[:, None, None, None]
    new_momentum = 0.9 * momentum + mean_delta
    new_params = (params.astype(jnp.float32) - 0.7 * (mean_delta + 0.9 * new_momentum)).astype(
        jnp.bfloat16
    )
    return (new_params, new_momentum)


def solution(mesh):
    return jax.shard_map(
        per_device,
        mesh=mesh,
        in_specs=(
            P(("path", "tensor"), None),
            P("path", None),
            P(None, None, ("tensor", "path"), None),
            P(None, None, ("tensor", "path"), None),
            P(),
            P(),
        ),
        out_specs=(
            P(None, None, ("tensor", "path"), None),
            P(None, None, ("tensor", "path"), None),
        ),
        check_vma=False,
    )
```

time: 421 us -> 452 us (1.074)
  the two profiles are of different devices: /device:TPU:1 before, /device:TPU:8 now
where the time goes in v1:
time: 452 us; the launch traced here: 451 us
  waiting for transfers between devices  321 us (71%)
  local copies, waits for them, and re-layouts  52.8 us (12%)
  matrix products  31.2 us (7%)
  starting transfers between devices  18.2 us (4%)
  between operations  13.9 us (3%)
  other arithmetic  13.5 us (3%)
    all_to_all x1, waiting for transfers between devices, per_device(): lax.all_to_all(jnp.moveaxis(deltas, 1, 0), 'path', split_axis=0, concat_a...  88.4 us
    all_to_all x1, waiting for transfers between devices, per_device(): lax.all_to_all(picked, 'path', split_axis=0, concat_axis=0, tiled=True)  86.8 us
    reduce_scatter x1, waiting for transfers between devices, per_device(): lax.psum_scatter(partial_out, 'tensor', scatter_dimension=0, tiled=True)  75 us
    all_gather x1, waiting for transfers between devices, per_device(): cotangent = lax.all_gather(own_cot, 'tensor', axis=0, tiled=True)  70.9 us
    all_to_all x1, starting transfers between devices, per_device(): lax.all_to_all(picked, 'path', split_axis=0, concat_axis=0, tiled=True)  10.4 us
    dot_general x1, matrix products, per_device(): lax.dot_general(weighting, got.reshape(path_count, -1), contract_first, p...  10.3 us
    another operation x3, local copies, waits for them, and re-layouts, per_device(): jnp.stack([gate_delta, up_delta, down_delta])  9.7 us
  transfers between devices with their start and end apart: 5, of which 4 were waited for; matrix products, arithmetic and copies ran while one was open for 3% of the time, Pallas kernels for 0%

profile of v1, /device:TPU:8, one launch (start us, length us, event | category | flops | bytes accessed | tf_op | source)
XLA Modules:
  0.0 450.7 jit_solution(17856748186250629865)
XLA Ops:
  8.5 4.6 %gather_fusion = bf16[32,3,14,2048]{3,2,1,0:T(8,128)(2,1)} fusion(bf16[3,3,14,2048]{3,2,1,0:T(8,128)(2,1)} %param.8, s32[1024]{0:T(1024)S(1)} %pad_clamp_fusion), kind=kCustom, calls=%fused_computation | custom fusion | bytes 11010176 | tf_op jit(solution)/shard_map/jit(_take)/gather | solution.py:19
  13.1 6.1 %broadcast_select_fusion = bf16[32,3,14,2048]{3,2,1,0:T(8,128)(2,1)} fusion(bf16[32,3,14,2048]{3,2,1,0:T(8,128)(2,1)} %gather_fusion, pred[32]{0:T(512)(128)(4,1)S(1)} %compare_and_fusion), kind=kLoop, calls=%fused_computation.2 | loop fusion | flops 2752512 | bytes 11010080 | tf_op jit(solution)/shard_map/jit(_take)/select_n | solution.py:19
  19.2 10.4 %all-to-all-start = ((bf16[32,3,14,2048]{3,2,1,0:T(8,128)(2,1)}), bf16[32,3,14,2048]{3,2,1,0:T(8,128)(2,1)}, u32[]{:S(2)}, u32[]{:S(2)}) async-start(bf16[32,3,14,2048]{3,2,1,0:T(8,128)(2,1)} %broadcast_select_fusion), calls=%async_computation | async-start | bytes 12582912 | tf_op jit(solution)/shard_map/all_to_all | solution.py:20
  29.8 0.7 fusion.9
  30.7 86.8 %all-to-all-done = bf16[32,3,14,2048]{3,2,1,0:T(8,128)(2,1)} async-done(((bf16[32,3,14,2048]{3,2,1,0:T(8,128)(2,1)}), bf16[32,3,14,2048]{3,2,1,0:T(8,128)(2,1)}, u32[]{:S(2)}, u32[]{:S(2)}) %all-to-all-start) | async-done | bytes 5505056 | tf_op jit(solution)/shard_map/all_to_all | solution.py:20
  117.5 5.9 %fusion.19 = (bf16[1,32,14,2048]{3,2,0,1:T(8,128)(2,1)S(1)}, bf16[1,32,14,2048]{3,2,0,1:T(8,128)(2,1)}, bf16[1,32,14,2048]{3,2,0,1:T(8,128)(2,1)}) fusion(bf16[3,32,14,2048]{3,2,0,1:T(8,128)(2,1)} %bitcast.2), kind=kLoop, calls=%fused_computation.41 | loop fusion | bytes 11010048 | tf_op jit(solution)/shard_map/slice | solution.py:23
  123.3 3.7 squeeze.9
  127.0 3.7 squeeze.10
  130.7 1.5 squeeze.11
  132.2 3.3 convolution_multiply_fusion.3
  135.5 2.0 multiply_convert_fusion.5
  137.5 2.7 convolution_multiply_fusion
  140.4 75.0 %reduce-scatter.2.cloned.1.call-done = f32[24,2048]{1,0:T(8,128)} async-done(((f32[384,2048]{1,0:T(8,128)}), f32[24,2048]{1,0:T(8,128)}) %reduce-scatter.2.cloned.1.call-update) | async-done | bytes 196624 | tf_op jit(solution)/shard_map/reduce_scatter | solution.py:38
  215.4 1.7 multiply_convert_fusion.8
  217.1 70.9 %all-gather.5.cloned.1.call-done = bf16[384,2048]{1,0:T(8,128)(2,1)} async-done(((bf16[24,2048]{1,0:T(8,128)(2,1)}), bf16[384,2048]{1,0:T(8,128)(2,1)}) %all-gather.5.cloned.1.call-update) | async-done | bytes 1572880 | tf_op jit(solution)/shard_map/all_gather | solution.py:43
  288.0 2.7 convolution_multiply_fusion.1
  290.7 0.8 copy-done.9
  291.5 2.5 multiply_convert_fusion.2
  294.1 2.5 stack.12
  296.6 4.0 multiply_convert_fusion.1
  300.6 3.6 stack.13
  304.2 3.8 multiply_convert_fusion
  307.9 3.6 stack.14
  311.6 3.4 maximum_bitcast_fusion
  315.0 3.2 copy.19
  318.2 7.5 %all-to-all-start.1 = ((bf16[32,3,14,2048]{3,2,1,0:T(8,128)(2,1)}), bf16[32,3,14,2048]{3,2,1,0:T(8,128)(2,1)}, u32[]{:S(2)}, u32[]{:S(2)}) async-start(bf16[32,3,14,2048]{3,2,1,0:T(8,128)(2,1)} %copy.19), calls=%async_computation.2 | async-start | bytes 12582912 | tf_op jit(solution)/shard_map/all_to_all | solution.py:69
  325.8 88.4 %all-to-all-done.1 = bf16[32,3,14,2048]{3,2,1,0:T(8,128)(2,1)} async-done(((bf16[32,3,14,2048]{3,2,1,0:T(8,128)(2,1)}), bf16[32,3,14,2048]{3,2,1,0:T(8,128)(2,1)}, u32[]{:S(2)}, u32[]{:S(2)}) %all-to-all-start.1) | async-done | bytes 5505056 | tf_op jit(solution)/shard_map/all_to_all | solution.py:69
  414.2 8.4 %reshape.41 = bf16[32,86016]{1,0:T(8,128)(2,1)} reshape(bf16[32,3,14,2048]{3,2,1,0:T(8,128)(2,1)} %all-to-all-done.1) | data formatting | bytes 11010048 | tf_op jit(solution)/shard_map/reshape | solution.py:73
  422.6 8.5 %dot_general.36 = bf16[3,14,2048,32]{2,1,0,3:T(8,128)(2,1)} reshape(bf16[86016,32]{0,1:T(8,128)(2,1)} %bitcast.31) | data formatting | bytes 11010048 | tf_op jit(solution)/shard_map/dot_general | solution.py:72
  431.0 10.3 %fusion.5 = (f32[3,3,14,2048]{3,0,2,1:T(4,128)S(1)}, bf16[3,3,14,2048]{3,0,2,1:T(4,128)(2,1)S(1)}) fusion(f32[3,3,14,2048]{3,2,1,0:T(8,128)S(1)} %copy-done.6, bf16[3,3,14,2048]{3,2,1,0:T(8,128)(2,1)S(1)} %copy-done, f32[3]{0:T(128)S(1)} %convert_element_type.59, bf16[3,14,2048,32]{2,1,0,3:T(8,128)(2,1)} %dot_general.36, s32[32]{0:T(128)S(1)} %copy-done.7, ...), kind=kOutput, calls=%fused_computation.11 | convolution fusion | flops 18837792 | bytes 8601868 | tf_op jit(solution)/shard_map/dot_general | solution.py:72
  441.4 1.6 copy.23
  443.0 1.2 copy.22
  (35 shorter events, 2.0 us)
Async XLA Ops:
  19.2 10.5 %copy-start.3 = (bf16[24,2048]{1,0:T(8,128)(2,1)S(1)}, bf16[24,2048]{1,0:T(8,128)(2,1)}, u32[]{:S(2)}) copy-start(bf16[24,2048]{1,0:T(8,128)(2,1)} %param.6) | copy-start | bytes 294916
  19.2 98.3 %all-to-all-start = ((bf16[32,3,14,2048]{3,2,1,0:T(8,128)(2,1)}), bf16[32,3,14,2048]{3,2,1,0:T(8,128)(2,1)}, u32[]{:S(2)}, u32[]{:S(2)}) async-start(bf16[32,3,14,2048]{3,2,1,0:T(8,128)(2,1)} %broadcast_select_fusion), calls=%async_computation | async-start | bytes 12582912 | tf_op jit(solution)/shard_map/all_to_all | solution.py:20
  29.6 102.6 %all-gather.3.cloned.1.call-start = ((), (), s32[]{:S(2)}) async-start(), calls=%async_computation.3 | async-start | bytes 1671168 | tf_op jit(solution)/shard_map/all_gather | solution.py:27
  30.6 184.8 %reduce-scatter.2.cloned.1.call-start = ((), (), s32[]{:S(2)}) async-start(), calls=%async_computation.4 | async-start | bytes 3342336 | tf_op jit(solution)/shard_map/reduce_scatter | solution.py:38
  132.2 3.3 copy-start.2
  132.2 3.3 copy-start.4
  135.5 2.0 copy-start.1
  140.2 147.8 %all-gather.5.cloned.1.call-start = ((), (), s32[]{:S(2)}) async-start(), calls=%async_computation.5 | async-start | bytes 1671168 | tf_op jit(solution)/shard_map/all_gather | solution.py:43
  288.0 3.5 copy-start.5
  288.0 3.5 copy-start.10
  290.7 0.8 copy-start.9
  318.2 7.5 %copy-start.7 = (s32[32]{0:T(128)S(1)}, s32[32]{0:T(128)}, u32[]{:S(2)}) copy-start(s32[32]{0:T(128)} %param.10) | copy-start | bytes 388
  318.2 7.5 %copy-start.8 = (s32[32]{0:T(128)S(1)}, s32[32]{0:T(128)}, u32[]{:S(2)}) copy-start(s32[32]{0:T(128)} %param.11) | copy-start | bytes 388
  318.2 96.0 %all-to-all-start.1 = ((bf16[32,3,14,2048]{3,2,1,0:T(8,128)(2,1)}), bf16[32,3,14,2048]{3,2,1,0:T(8,128)(2,1)}, u32[]{:S(2)}, u32[]{:S(2)}) async-start(bf16[32,3,14,2048]{3,2,1,0:T(8,128)(2,1)} %copy.19), calls=%async_computation.2 | async-start | bytes 12582912 | tf_op jit(solution)/shard_map/all_to_all | solution.py:69
  422.6 8.5 %copy-start = (bf16[3,3,14,2048]{3,2,1,0:T(8,128)(2,1)S(1)}, bf16[3,3,14,2048]{3,2,1,0:T(8,128)(2,1)}, u32[]{:S(2)}) copy-start(bf16[3,3,14,2048]{3,2,1,0:T(8,128)(2,1)} %param.8) | copy-start | bytes 1548292
  422.6 8.5 %copy-start.6 = (f32[3,3,14,2048]{3,2,1,0:T(8,128)S(1)}, f32[3,3,14,2048]{3,2,1,0:T(8,128)}, u32[]{:S(2)}) copy-start(f32[3,3,14,2048]{3,2,1,0:T(8,128)} %param.9) | copy-start | bytes 3096580
Sparse Core Ops, SparseCore 0:
  33.1 73.2 all-gather.2
  140.3 75.0 reduce-scatter.1
  218.1 69.8 all-gather.4

commit v2 on v0

--- a/solution.py
+++ b/solution.py
@@ -14,6 +14,24 @@
     return lax.dot_general(
         weighting, flat, (((0,), (0,)), ((), ())), preferred_element_type=jnp.float32
     )
+
+
+def ring_gather(x, axis, size):
+    fwd = [(i, (i + 1) % size) for i in range(size)]
+    bwd = [(i, (i - 1) % size) for i in range(size)]
+    parts = [None] * size
+    parts[0] = x
+    ahead = x
+    behind = x
+    for k in range(1, size // 2 + 1):
+        ahead = lax.ppermute(ahead, axis, fwd)
+        parts[k] = ahead
+        if k < size - k:
+            behind = lax.ppermute(behind, axis, bwd)
+            parts[size - k] = behind
+    rev = jnp.stack([parts[(-k) % size] for k in range(size)])
+    ordered = jnp.roll(rev, lax.axis_index(axis), axis=0)
+    return ordered.reshape(size * x.shape[0], x.shape[1])
 
 
 def per_device(hidden_in, teacher, params, momentum, path_alive, path_module):
@@ -35,9 +53,10 @@
     gate_rows = gate_rows.reshape(local_rows, width)
     up_rows = up_rows.reshape(local_rows, width)
     down_rows = down_rows.reshape(local_rows, width)
-    rows_in = lax.all_gather(hidden_in, "tensor", axis=0, tiled=True)
-    mean_sq = jnp.mean(jnp.square(rows_in.astype(jnp.float32)), axis=1, keepdims=True)
-    normed = (rows_in.astype(jnp.float32) * lax.rsqrt(mean_sq + 1e-05)).astype(jnp.bfloat16)
+    own = hidden_in.astype(jnp.float32)
+    mean_sq = jnp.mean(jnp.square(own), axis=1, keepdims=True)
+    own_normed = (own * lax.rsqrt(mean_sq + 1e-05)).astype(jnp.bfloat16)
+    normed = lax.all_gather(own_normed, "tensor", axis=0, tiled=True)
     gate_pre = lax.dot_general(
         normed, gate_rows, contract_last, preferred_element_type=jnp.float32
     ) / math.sqrt(D)
@@ -48,8 +67,12 @@
     activated = gate_pre * sigmoid_gate
     hidden = (activated * up_proj).astype(jnp.bfloat16)
     partial_out = jnp.dot(hidden, down_rows, preferred_element_type=jnp.float32) / math.sqrt(FW)
-    output = lax.psum(partial_out, "tensor")
-    cotangent = (4.0 * (output - teacher.astype(jnp.float32))).astype(jnp.bfloat16)
+    out_rows = lax.psum_scatter(partial_out, "tensor", scatter_dimension=0, tiled=True)
+    own_count = out_rows.shape[0]
+    start = lax.axis_index("tensor") * own_count
+    target = lax.dynamic_slice_in_dim(teacher, start, own_count, 0)
+    own_cot = (4.0 * (out_rows - target.astype(jnp.float32))).astype(jnp.bfloat16)
+    cotangent = ring_gather(own_cot, "tensor", teacher.shape[0] // own_count)
     down_delta = (
         lax.dot_general(hidden, cotangent, contract_first, preferred_element_type=jnp.float32)
         / math.sqrt(FW)

time: 421 us -> 433 us (1.029)
  starting transfers between devices: 36.3 us -> 99.2 us
  waiting for transfers between devices: 270 us -> 232 us
  blocking collectives: 37.7 us -> 0 us
  local copies, waits for them, and re-layouts: 23 us -> 48.1 us
    psum x1 -> x0, waiting for transfers between devices: 147 us -> none  [per_device(): output = lax.psum(partial_out, 'tensor')]
    reduce_scatter x0 -> x1, waiting for transfers between devices: none -> 74.5 us  [per_device(): lax.psum_scatter(partial_out, 'tensor', scatter_dimension=0, tiled=True)]
    ppermute x0 -> x15, starting transfers between devices: none -> 45.2 us  [the longest x7 29.1 us: ring_gather(): behind = lax.ppermute(behind, axis, bwd)]
    all_to_all x1 -> x0, blocking collectives: 37.7 us -> none  [per_device(): lax.all_to_all(gate_pick, 'path', split_axis=0, concat_axis=0, tiled=True)]
    all_to_all x0 -> x1, waiting for transfers between devices: none -> 28.3 us  [per_device(): lax.all_to_all(gate_pick, 'path', split_axis=0, concat_axis=0, tiled=True)]
    unnamed x30 -> x54, local copies, waits for them, and re-layouts: 4.47 us -> 23.3 us
    all_to_all x0 -> x1, starting transfers between devices: none -> 10.6 us  [per_device(): lax.all_to_all(gate_pick, 'path', split_axis=0, concat_axis=0, tiled=True)]
    ppermute x0 -> x15, waiting for transfers between devices: none -> 9.8 us  [the longest x8 9.07 us: ring_gather(): ahead = lax.ppermute(ahead, axis, fwd)]
  transfers between devices with their start and end apart: 7 -> 23, of which waited for: 7 -> 11; matrix products, arithmetic and copies ran while one was open for 6% -> 8% of each run, Pallas kernels for 0% -> 0%
where the time goes in v2:
time: 433 us; the launch traced here: 432 us
  waiting for transfers between devices  232 us (54%)
  starting transfers between devices  99.2 us (23%)
  local copies, waits for them, and re-layouts  48.1 us (11%)
  matrix products  27.6 us (6%)
  between operations  14.5 us (3%)
  other arithmetic  10.8 us (2%)
    reduce_scatter x1, waiting for transfers between devices, per_device(): lax.psum_scatter(partial_out, 'tensor', scatter_dimension=0, tiled=True)  74.5 us
    ppermute x7, starting transfers between devices, ring_gather(): behind = lax.ppermute(behind, axis, bwd)  29.1 us
    all_to_all x1, waiting for transfers between devices, per_device(): lax.all_to_all(gate_pick, 'path', split_axis=0, concat_axis=0, tiled=True)  28.3 us
    all_to_all x1, waiting for transfers between devices, per_device(): lax.all_to_all(up_pick, 'path', split_axis=0, concat_axis=0, tiled=True)  27.7 us
    unnamed x54, local copies, waits for them, and re-layouts  23.3 us
    all_to_all x1, waiting for transfers between devices, per_device(): lax.all_to_all(down_pick, 'path', split_axis=0, concat_axis=0, tiled=True)  23.1 us
    all_to_all x1, starting transfers between devices, per_device(): lax.all_to_all(gate_delta.reshape(piece_shape), 'path', split_axis=0, con...  22.6 us
    all_to_all x1, waiting for transfers between devices, per_device(): lax.all_to_all(down_delta.reshape(piece_shape), 'path', split_axis=0, con...  22.5 us
  transfers between devices with their start and end apart: 23, of which 11 were waited for; matrix products, arithmetic and copies ran while one was open for 8% of the time, Pallas kernels for 0%

profile of v2, /device:TPU:1, one launch (start us, length us, event | category | flops | bytes accessed | tf_op | source)
XLA Modules:
  0.0 431.7 jit_solution(18142872696267785733)
XLA Ops:
  14.4 5.1 %broadcast_select_fusion = (bf16[32,14,2048]{2,1,0:T(8,128)(2,1)}, bf16[32,14,2048]{2,1,0:T(8,128)(2,1)}, bf16[32,14,2048]{2,1,0:T(8,128)(2,1)}) fusion(bf16[32,14,2048]{2,1,0:T(8,128)(2,1)} %gather_fusion.2, pred[32]{0:T(512)(128)(4,1)S(1)} %compare_and_fusion, bf16[32,14,2048]{2,1,0:T(8,128)(2,1)} %gather_fusion.1, bf16[32,14,2048]{2,1,0:T(8,128)(2,1)S(1)} %gather_fusion), kind=kLoop, calls=%fused_computation.10 | loop fusion | flops 2752512 | bytes 11010080 | tf_op jit(solution)/shard_map/jit(_take)/select_n | solution.py:46
  19.5 10.6 %all-to-all-start = ((bf16[32,14,2048]{2,1,0:T(8,128)(2,1)}), bf16[32,14,2048]{2,1,0:T(8,128)(2,1)S(1)}, u32[]{:S(2)}, u32[]{:S(2)}) async-start(bf16[32,14,2048]{2,1,0:T(8,128)(2,1)} %get-tuple-element.16), calls=%async_computation | async-start | bytes 4194304 | tf_op jit(solution)/shard_map/all_to_all | solution.py:48
  30.3 28.3 %all-to-all-done = bf16[32,14,2048]{2,1,0:T(8,128)(2,1)S(1)} async-done(((bf16[32,14,2048]{2,1,0:T(8,128)(2,1)}), bf16[32,14,2048]{2,1,0:T(8,128)(2,1)S(1)}, u32[]{:S(2)}, u32[]{:S(2)}) %all-to-all-start) | async-done | bytes 1835040 | tf_op jit(solution)/shard_map/all_to_all | solution.py:48
  58.6 5.2 %all-to-all-start.1 = ((bf16[32,14,2048]{2,1,0:T(8,128)(2,1)}), bf16[32,14,2048]{2,1,0:T(8,128)(2,1)}, u32[]{:S(2)}, u32[]{:S(2)}) async-start(bf16[32,14,2048]{2,1,0:T(8,128)(2,1)} %get-tuple-element.15), calls=%async_computation.1 | async-start | bytes 4194304 | tf_op jit(solution)/shard_map/all_to_all | solution.py:49
  64.6 27.7 %all-to-all-done.1 = bf16[32,14,2048]{2,1,0:T(8,128)(2,1)} async-done(((bf16[32,14,2048]{2,1,0:T(8,128)(2,1)}), bf16[32,14,2048]{2,1,0:T(8,128)(2,1)}, u32[]{:S(2)}, u32[]{:S(2)}) %all-to-all-start.1) | async-done | bytes 1835040 | tf_op jit(solution)/shard_map/all_to_all | solution.py:49
  92.3 5.2 %all-to-all-start.2 = ((bf16[32,14,2048]{2,1,0:T(8,128)(2,1)}), bf16[32,14,2048]{2,1,0:T(8,128)(2,1)}, u32[]{:S(2)}, u32[]{:S(2)}) async-start(bf16[32,14,2048]{2,1,0:T(8,128)(2,1)} %get-tuple-element.14), calls=%async_computation.2 | async-start | bytes 4194304 | tf_op jit(solution)/shard_map/all_to_all | solution.py:50
  99.1 3.7 reshape.78
  102.8 23.1 %all-to-all-done.2 = bf16[32,14,2048]{2,1,0:T(8,128)(2,1)} async-done(((bf16[32,14,2048]{2,1,0:T(8,128)(2,1)}), bf16[32,14,2048]{2,1,0:T(8,128)(2,1)}, u32[]{:S(2)}, u32[]{:S(2)}) %all-to-all-start.2) | async-done | bytes 1835040 | tf_op jit(solution)/shard_map/all_to_all | solution.py:50
  128.5 3.9 all-gather.2.cloned.1.call-done
  132.4 3.3 convolution_multiply_fusion.3
  140.3 74.5 %reduce-scatter.2.cloned.1.call-done = f32[24,2048]{1,0:T(8,128)} async-done(((f32[384,2048]{1,0:T(8,128)}), f32[24,2048]{1,0:T(8,128)}) %reduce-scatter.2.cloned.1.call-update) | async-done | bytes 196624 | tf_op jit(solution)/shard_map/reduce_scatter | solution.py:70
  219.1 2.7 collective-permute-start.7
  222.5 3.7 collective-permute-start.1
  228.8 4.6 %collective-permute-start.2 = (bf16[24,2048]{1,0:T(8,128)(2,1)S(1)}, bf16[24,2048]{1,0:T(8,128)(2,1)S(1)}, u32[]{:S(2)}, u32[]{:S(2)}) collective-permute-start(bf16[24,2048]{1,0:T(8,128)(2,1)S(1)} %collective-permute-done.1), channel_id=1, source_target_pairs={{0,15},{1,0},{2,1},{3,2},{4,3},{5,4},{6,5},{7,6},{8,7},{9,8},{10,9... | collective-permute-start | bytes 294920 | tf_op jit(solution)/shard_map/ppermute | solution.py:30
  235.9 4.6 %collective-permute-start.3 = (bf16[24,2048]{1,0:T(8,128)(2,1)S(1)}, bf16[24,2048]{1,0:T(8,128)(2,1)S(1)}, u32[]{:S(2)}, u32[]{:S(2)}) collective-permute-start(bf16[24,2048]{1,0:T(8,128)(2,1)S(1)} %collective-permute-done.2), channel_id=1, source_target_pairs={{0,15},{1,0},{2,1},{3,2},{4,3},{5,4},{6,5},{7,6},{8,7},{9,8},{10,9... | collective-permute-start | bytes 294920 | tf_op jit(solution)/shard_map/ppermute | solution.py:30
  243.1 4.6 %collective-permute-start.4 = (bf16[24,2048]{1,0:T(8,128)(2,1)S(1)}, bf16[24,2048]{1,0:T(8,128)(2,1)S(1)}, u32[]{:S(2)}, u32[]{:S(2)}) collective-permute-start(bf16[24,2048]{1,0:T(8,128)(2,1)S(1)} %collective-permute-done.3), channel_id=1, source_target_pairs={{0,15},{1,0},{2,1},{3,2},{4,3},{5,4},{6,5},{7,6},{8,7},{9,8},{10,9... | collective-permute-start | bytes 294920 | tf_op jit(solution)/shard_map/ppermute | solution.py:30
  250.3 4.6 %collective-permute-start.5 = (bf16[24,2048]{1,0:T(8,128)(2,1)S(1)}, bf16[24,2048]{1,0:T(8,128)(2,1)S(1)}, u32[]{:S(2)}, u32[]{:S(2)}) collective-permute-start(bf16[24,2048]{1,0:T(8,128)(2,1)S(1)} %collective-permute-done.4), channel_id=1, source_target_pairs={{0,15},{1,0},{2,1},{3,2},{4,3},{5,4},{6,5},{7,6},{8,7},{9,8},{10,9... | collective-permute-start | bytes 294920 | tf_op jit(solution)/shard_map/ppermute | solution.py:30
  257.4 4.6 %collective-permute-start.6 = (bf16[24,2048]{1,0:T(8,128)(2,1)S(1)}, bf16[24,2048]{1,0:T(8,128)(2,1)S(1)}, u32[]{:S(2)}, u32[]{:S(2)}) collective-permute-start(bf16[24,2048]{1,0:T(8,128)(2,1)S(1)} %collective-permute-done.5), channel_id=1, source_target_pairs={{0,15},{1,0},{2,1},{3,2},{4,3},{5,4},{6,5},{7,6},{8,7},{9,8},{10,9... | collective-permute-start | bytes 294920 | tf_op jit(solution)/shard_map/ppermute | solution.py:30
  264.6 4.0 collective-permute-done.13
  271.2 5.1 %collective-permute-done.14 = bf16[24,2048]{1,0:T(8,128)(2,1)S(1)} collective-permute-done((bf16[24,2048]{1,0:T(8,128)(2,1)S(1)}, bf16[24,2048]{1,0:T(8,128)(2,1)S(1)}, u32[]{:S(2)}, u32[]{:S(2)}) %collective-permute-start.14) | collective-permute-done | bytes 98336 | tf_op jit(solution)/shard_map/ppermute | solution.py:27
  298.4 22.6 %all-to-all-start.3 = ((bf16[32,14,2048]{2,1,0:T(8,128)(2,1)}), bf16[32,14,2048]{2,1,0:T(8,128)(2,1)S(1)}, u32[]{:S(2)}, u32[]{:S(2)}) async-start(bf16[32,14,2048]{2,1,0:T(8,128)(2,1)} %reshape.81), calls=%async_computation.4 | async-start | bytes 4194304 | tf_op jit(solution)/shard_map/all_to_all | solution.py:102
  321.0 4.0 multiply_convert_fusion.1
  325.1 3.6 reshape.84
  328.7 20.7 %all-to-all-done.3 = bf16[32,14,2048]{2,1,0:T(8,128)(2,1)S(1)} async-done(((bf16[32,14,2048]{2,1,0:T(8,128)(2,1)}), bf16[32,14,2048]{2,1,0:T(8,128)(2,1)S(1)}, u32[]{:S(2)}, u32[]{:S(2)}) %all-to-all-start.3) | async-done | bytes 1835040 | tf_op jit(solution)/shard_map/all_to_all | solution.py:102
  349.4 5.2 %all-to-all-start.4 = ((bf16[32,14,2048]{2,1,0:T(8,128)(2,1)}), bf16[32,14,2048]{2,1,0:T(8,128)(2,1)}, u32[]{:S(2)}, u32[]{:S(2)}) async-start(bf16[32,14,2048]{2,1,0:T(8,128)(2,1)} %reshape.84), calls=%async_computation.5 | async-start | bytes 4194304 | tf_op jit(solution)/shard_map/all_to_all | solution.py:105
  354.5 3.8 multiply_convert_fusion
  358.4 3.6 reshape.87
  362.0 21.0 %all-to-all-done.4 = bf16[32,14,2048]{2,1,0:T(8,128)(2,1)} async-done(((bf16[32,14,2048]{2,1,0:T(8,128)(2,1)}), bf16[32,14,2048]{2,1,0:T(8,128)(2,1)}, u32[]{:S(2)}, u32[]{:S(2)}) %all-to-all-start.4) | async-done | bytes 1835040 | tf_op jit(solution)/shard_map/all_to_all | solution.py:105
  383.0 5.2 %all-to-all-start.5 = ((bf16[32,14,2048]{2,1,0:T(8,128)(2,1)}), bf16[32,14,2048]{2,1,0:T(8,128)(2,1)}, u32[]{:S(2)}, u32[]{:S(2)}) async-start(bf16[32,14,2048]{2,1,0:T(8,128)(2,1)} %reshape.87), calls=%async_computation.6 | async-start | bytes 4194304 | tf_op jit(solution)/shard_map/all_to_all | solution.py:108
  390.4 3.8 convolution_bitcast_fusion.1
  394.2 22.5 %all-to-all-done.5 = bf16[32,14,2048]{2,1,0:T(8,128)(2,1)} async-done(((bf16[32,14,2048]{2,1,0:T(8,128)(2,1)}), bf16[32,14,2048]{2,1,0:T(8,128)(2,1)}, u32[]{:S(2)}, u32[]{:S(2)}) %all-to-all-start.5) | async-done | bytes 1835040 | tf_op jit(solution)/shard_map/all_to_all | solution.py:108
  416.7 3.6 convolution_bitcast_fusion
  (103 shorter events, 68.8 us)
Async XLA Ops:
  19.5 10.6 %copy-start.4 = (bf16[24,2048]{1,0:T(8,128)(2,1)S(1)}, bf16[24,2048]{1,0:T(8,128)(2,1)}, u32[]{:S(2)}) copy-start(bf16[24,2048]{1,0:T(8,128)(2,1)} %param.8) | copy-start | bytes 294916
  19.5 39.1 %all-to-all-start = ((bf16[32,14,2048]{2,1,0:T(8,128)(2,1)}), bf16[32,14,2048]{2,1,0:T(8,128)(2,1)S(1)}, u32[]{:S(2)}, u32[]{:S(2)}) async-start(bf16[32,14,2048]{2,1,0:T(8,128)(2,1)} %get-tuple-element.16), calls=%async_computation | async-start | bytes 4194304 | tf_op jit(solution)/shard_map/all_to_all | solution.py:48
  58.6 33.7 %all-to-all-start.1 = ((bf16[32,14,2048]{2,1,0:T(8,128)(2,1)}), bf16[32,14,2048]{2,1,0:T(8,128)(2,1)}, u32[]{:S(2)}, u32[]{:S(2)}) async-start(bf16[32,14,2048]{2,1,0:T(8,128)(2,1)} %get-tuple-element.15), calls=%async_computation.1 | async-start | bytes 4194304 | tf_op jit(solution)/shard_map/all_to_all | solution.py:49
  63.8 68.6 %all-gather.2.cloned.1.call-start = ((), (), s32[]{:S(2)}) async-start(), calls=%async_computation.7 | async-start | bytes 1671168 | tf_op jit(solution)/shard_map/all_gather | solution.py:59
  92.3 33.6 %all-to-all-start.2 = ((bf16[32,14,2048]{2,1,0:T(8,128)(2,1)}), bf16[32,14,2048]{2,1,0:T(8,128)(2,1)}, u32[]{:S(2)}, u32[]{:S(2)}) async-start(bf16[32,14,2048]{2,1,0:T(8,128)(2,1)} %get-tuple-element.14), calls=%async_computation.2 | async-start | bytes 4194304 | tf_op jit(solution)/shard_map/all_to_all | solution.py:50
  97.4 117.4 %reduce-scatter.2.cloned.1.call-start = ((), (), s32[]{:S(2)}) async-start(), calls=%async_computation.8 | async-start | bytes 3342336 | tf_op jit(solution)/shard_map/reduce_scatter | solution.py:70
  132.4 3.3 copy-start.1
  132.4 3.3 copy-start.5
  216.5 6.0 %collective-permute-start = (bf16[24,2048]{1,0:T(8,128)(2,1)S(1)}, bf16[24,2048]{1,0:T(8,128)(2,1)S(1)}, u32[]{:S(2)}, u32[]{:S(2)}) collective-permute-start(bf16[24,2048]{1,0:T(8,128)(2,1)S(1)} %get-tuple-element.8), channel_id=1, source_target_pairs={{0,15},{1,0},{2,1},{3,2},{4,3},{5,4},{6,5},{7,6},{8,7},{9,8},{10,9... | collective-permute-start | bytes 294920 | tf_op jit(solution)/shard_map/ppermute | solution.py:30
  219.1 7.1 %collective-permute-start.7 = (bf16[24,2048]{1,0:T(8,128)(2,1)S(1)}, bf16[24,2048]{1,0:T(8,128)(2,1)S(1)}, u32[]{:S(2)}, u32[]{:S(2)}) collective-permute-start(bf16[24,2048]{1,0:T(8,128)(2,1)S(1)} %get-tuple-element.8), channel_id=1, source_target_pairs={{0,1},{1,2},{2,3},{3,4},{4,5},{5,6},{6,7},{7,8},{8,9},{9,10},{10,1... | collective-permute-start | bytes 294920 | tf_op jit(solution)/shard_map/ppermute | solution.py:27
  222.5 6.3 %collective-permute-start.1 = (bf16[24,2048]{1,0:T(8,128)(2,1)S(1)}, bf16[24,2048]{1,0:T(8,128)(2,1)S(1)}, u32[]{:S(2)}, u32[]{:S(2)}) collective-permute-start(bf16[24,2048]{1,0:T(8,128)(2,1)S(1)} %collective-permute-done), channel_id=1, source_target_pairs={{0,15},{1,0},{2,1},{3,2},{4,3},{5,4},{6,5},{7,6},{8,7},{9,8},{10,9... | collective-permute-start | bytes 294920 | tf_op jit(solution)/shard_map/ppermute | solution.py:30
  226.2 7.1 %collective-permute-start.8 = (bf16[24,2048]{1,0:T(8,128)(2,1)S(1)}, bf16[24,2048]{1,0:T(8,128)(2,1)S(1)}, u32[]{:S(2)}, u32[]{:S(2)}) collective-permute-start(bf16[24,2048]{1,0:T(8,128)(2,1)S(1)} %collective-permute-done.7), channel_id=1, source_target_pairs={{0,1},{1,2},{2,3},{3,4},{4,5},{5,6},{6,7},{7,8},{8,9},{9,10},{10,1... | collective-permute-start | bytes 294920 | tf_op jit(solution)/shard_map/ppermute | solution.py:27
  228.8 7.2 %collective-permute-start.2 = (bf16[24,2048]{1,0:T(8,128)(2,1)S(1)}, bf16[24,2048]{1,0:T(8,128)(2,1)S(1)}, u32[]{:S(2)}, u32[]{:S(2)}) collective-permute-start(bf16[24,2048]{1,0:T(8,128)(2,1)S(1)} %collective-permute-done.1), channel_id=1, source_target_pairs={{0,15},{1,0},{2,1},{3,2},{4,3},{5,4},{6,5},{7,6},{8,7},{9,8},{10,9... | collective-permute-start | bytes 294920 | tf_op jit(solution)/shard_map/ppermute | solution.py:30
  233.4 7.1 %collective-permute-start.9 = (bf16[24,2048]{1,0:T(8,128)(2,1)S(1)}, bf16[24,2048]{1,0:T(8,128)(2,1)S(1)}, u32[]{:S(2)}, u32[]{:S(2)}) collective-permute-start(bf16[24,2048]{1,0:T(8,128)(2,1)S(1)} %collective-permute-done.8), channel_id=1, source_target_pairs={{0,1},{1,2},{2,3},{3,4},{4,5},{5,6},{6,7},{7,8},{8,9},{9,10},{10,1... | collective-permute-start | bytes 294920 | tf_op jit(solution)/shard_map/ppermute | solution.py:27
  235.9 7.2 %collective-permute-start.3 = (bf16[24,2048]{1,0:T(8,128)(2,1)S(1)}, bf16[24,2048]{1,0:T(8,128)(2,1)S(1)}, u32[]{:S(2)}, u32[]{:S(2)}) collective-permute-start(bf16[24,2048]{1,0:T(8,128)(2,1)S(1)} %collective-permute-done.2), channel_id=1, source_target_pairs={{0,15},{1,0},{2,1},{3,2},{4,3},{5,4},{6,5},{7,6},{8,7},{9,8},{10,9... | collective-permute-start | bytes 294920 | tf_op jit(solution)/shard_map/ppermute | solution.py:30
  240.5 7.2 %collective-permute-start.10 = (bf16[24,2048]{1,0:T(8,128)(2,1)S(1)}, bf16[24,2048]{1,0:T(8,128)(2,1)S(1)}, u32[]{:S(2)}, u32[]{:S(2)}) collective-permute-start(bf16[24,2048]{1,0:T(8,128)(2,1)S(1)} %collective-permute-done.9), channel_id=1, source_target_pairs={{0,1},{1,2},{2,3},{3,4},{4,5},{5,6},{6,7},{7,8},{8,9},{9,10},{10,1... | collective-permute-start | bytes 294920 | tf_op jit(solution)/shard_map/ppermute | solution.py:27
  243.1 7.2 %collective-permute-start.4 = (bf16[24,2048]{1,0:T(8,128)(2,1)S(1)}, bf16[24,2048]{1,0:T(8,128)(2,1)S(1)}, u32[]{:S(2)}, u32[]{:S(2)}) collective-permute-start(bf16[24,2048]{1,0:T(8,128)(2,1)S(1)} %collective-permute-done.3), channel_id=1, source_target_pairs={{0,15},{1,0},{2,1},{3,2},{4,3},{5,4},{6,5},{7,6},{8,7},{9,8},{10,9... | collective-permute-start | bytes 294920 | tf_op jit(solution)/shard_map/ppermute | solution.py:30
  247.7 7.1 %collective-permute-start.11 = (bf16[24,2048]{1,0:T(8,128)(2,1)S(1)}, bf16[24,2048]{1,0:T(8,128)(2,1)S(1)}, u32[]{:S(2)}, u32[]{:S(2)}) collective-permute-start(bf16[24,2048]{1,0:T(8,128)(2,1)S(1)} %collective-permute-done.10), channel_id=1, source_target_pairs={{0,1},{1,2},{2,3},{3,4},{4,5},{5,6},{6,7},{7,8},{8,9},{9,10},{10,1... | collective-permute-start | bytes 294920 | tf_op jit(solution)/shard_map/ppermute | solution.py:27
  250.3 7.2 %collective-permute-start.5 = (bf16[24,2048]{1,0:T(8,128)(2,1)S(1)}, bf16[24,2048]{1,0:T(8,128)(2,1)S(1)}, u32[]{:S(2)}, u32[]{:S(2)}) collective-permute-start(bf16[24,2048]{1,0:T(8,128)(2,1)S(1)} %collective-permute-done.4), channel_id=1, source_target_pairs={{0,15},{1,0},{2,1},{3,2},{4,3},{5,4},{6,5},{7,6},{8,7},{9,8},{10,9... | collective-permute-start | bytes 294920 | tf_op jit(solution)/shard_map/ppermute | solution.py:30
  254.8 7.2 %collective-permute-start.12 = (bf16[24,2048]{1,0:T(8,128)(2,1)S(1)}, bf16[24,2048]{1,0:T(8,128)(2,1)S(1)}, u32[]{:S(2)}, u32[]{:S(2)}) collective-permute-start(bf16[24,2048]{1,0:T(8,128)(2,1)S(1)} %collective-permute-done.11), channel_id=1, source_target_pairs={{0,1},{1,2},{2,3},{3,4},{4,5},{5,6},{6,7},{7,8},{8,9},{9,10},{10,1... | collective-permute-start | bytes 294920 | tf_op jit(solution)/shard_map/ppermute | solution.py:27
  257.4 13.1 %collective-permute-start.6 = (bf16[24,2048]{1,0:T(8,128)(2,1)S(1)}, bf16[24,2048]{1,0:T(8,128)(2,1)S(1)}, u32[]{:S(2)}, u32[]{:S(2)}) collective-permute-start(bf16[24,2048]{1,0:T(8,128)(2,1)S(1)} %collective-permute-done.5), channel_id=1, source_target_pairs={{0,15},{1,0},{2,1},{3,2},{4,3},{5,4},{6,5},{7,6},{8,7},{9,8},{10,9... | collective-permute-start | bytes 294920 | tf_op jit(solution)/shard_map/ppermute | solution.py:30
  262.0 6.6 %collective-permute-start.13 = (bf16[24,2048]{1,0:T(8,128)(2,1)S(1)}, bf16[24,2048]{1,0:T(8,128)(2,1)S(1)}, u32[]{:S(2)}, u32[]{:S(2)}) collective-permute-start(bf16[24,2048]{1,0:T(8,128)(2,1)S(1)} %collective-permute-done.12), channel_id=1, source_target_pairs={{0,1},{1,2},{2,3},{3,4},{4,5},{5,6},{6,7},{7,8},{8,9},{9,10},{10,1... | collective-permute-start | bytes 294920 | tf_op jit(solution)/shard_map/ppermute | solution.py:27
  268.6 7.6 %collective-permute-start.14 = (bf16[24,2048]{1,0:T(8,128)(2,1)S(1)}, bf16[24,2048]{1,0:T(8,128)(2,1)S(1)}, u32[]{:S(2)}, u32[]{:S(2)}) collective-permute-start(bf16[24,2048]{1,0:T(8,128)(2,1)S(1)} %collective-permute-done.13), channel_id=1, source_target_pairs={{0,1},{1,2},{2,3},{3,4},{4,5},{5,6},{6,7},{7,8},{8,9},{9,10},{10,1... | collective-permute-start | bytes 294920 | tf_op jit(solution)/shard_map/ppermute | solution.py:27
  293.3 2.1 copy-start.6
  293.3 2.2 copy-start.10
  298.4 50.9 %all-to-all-start.3 = ((bf16[32,14,2048]{2,1,0:T(8,128)(2,1)}), bf16[32,14,2048]{2,1,0:T(8,128)(2,1)S(1)}, u32[]{:S(2)}, u32[]{:S(2)}) async-start(bf16[32,14,2048]{2,1,0:T(8,128)(2,1)} %reshape.81), calls=%async_computation.4 | async-start | bytes 4194304 | tf_op jit(solution)/shard_map/all_to_all | solution.py:102
  349.4 33.7 %all-to-all-start.4 = ((bf16[32,14,2048]{2,1,0:T(8,128)(2,1)}), bf16[32,14,2048]{2,1,0:T(8,128)(2,1)}, u32[]{:S(2)}, u32[]{:S(2)}) async-start(bf16[32,14,2048]{2,1,0:T(8,128)(2,1)} %reshape.84), calls=%async_computation.5 | async-start | bytes 4194304 | tf_op jit(solution)/shard_map/all_to_all | solution.py:105
  362.0 26.2 %copy-start.7 = (s32[32]{0:T(128)S(1)}, s32[32]{0:T(128)}, u32[]{:S(2)}) copy-start(s32[32]{0:T(128)} %param.12) | copy-start | bytes 388
  362.0 26.2 %copy-start.8 = (s32[32]{0:T(128)S(1)}, s32[32]{0:T(128)}, u32[]{:S(2)}) copy-start(s32[32]{0:T(128)} %param.13) | copy-start | bytes 388
  383.0 33.6 %all-to-all-start.5 = ((bf16[32,14,2048]{2,1,0:T(8,128)(2,1)}), bf16[32,14,2048]{2,1,0:T(8,128)(2,1)}, u32[]{:S(2)}, u32[]{:S(2)}) async-start(bf16[32,14,2048]{2,1,0:T(8,128)(2,1)} %reshape.87), calls=%async_computation.6 | async-start | bytes 4194304 | tf_op jit(solution)/shard_map/all_to_all | solution.py:108
  390.4 29.9 %copy-start = (bf16[3,3,14,2048]{3,2,1,0:T(8,128)(2,1)S(1)}, bf16[3,3,14,2048]{3,2,1,0:T(8,128)(2,1)}, u32[]{:S(2)}) copy-start(bf16[3,3,14,2048]{3,2,1,0:T(8,128)(2,1)} %param.10) | copy-start | bytes 1548292
  390.4 29.9 %copy-start.3 = (f32[3,3,14,2048]{3,2,1,0:T(8,128)S(1)}, f32[3,3,14,2048]{3,2,1,0:T(8,128)}, u32[]{:S(2)}) copy-start(f32[3,3,14,2048]{3,2,1,0:T(8,128)} %param.11) | copy-start | bytes 3096580
  (2 other events, 2.1 us)
Sparse Core Ops, SparseCore 0:
  67.2 65.0 all-gather.1
  140.4 74.3 reduce-scatter.1

commit v3 on v1

v3 whole, which is shorter than its diff:
```python
import math

import jax
import jax.numpy as jnp
from jax import lax
from jax.sharding import PartitionSpec as P

D = 2048
FW = 7168


def per_device(hidden_in, teacher, params, momentum, path_alive, path_module):
    module_count = params.shape[0]
    block_rows = params.shape[2]
    width = params.shape[3]
    path_count = path_alive.shape[0]
    picked = jnp.take(params, path_module, axis=0)
    rows = lax.all_to_all(picked, "path", split_axis=0, concat_axis=0, tiled=True)
    own = hidden_in.astype(jnp.float32)
    mean_sq = jnp.mean(jnp.square(own), axis=1, keepdims=True)
    own_normed = (own * lax.rsqrt(mean_sq + 1e-05)).astype(jnp.bfloat16)
    normed = lax.all_gather(own_normed, "tensor", axis=0, tiled=True)
    proj = lax.dot_general(
        normed, rows, (((1,), (3,)), ((), ())), preferred_element_type=jnp.float32
    ) / math.sqrt(D)
    gate_pre = proj[:, :, 0, :]
    up_proj = proj[:, :, 1, :]
    down_rows = rows[:, 2]
    sigmoid_gate = jax.nn.sigmoid(gate_pre)
    activated = gate_pre * sigmoid_gate
    hidden = (activated * up_proj).astype(jnp.bfloat16)
    partial_out = lax.dot_general(
        hidden, down_rows, (((1, 2), (0, 1)), ((), ())), preferred_element_type=jnp.float32
    ) / math.sqrt(FW)
    output = lax.psum(partial_out, "tensor")
    cotangent = (4.0 * (output - teacher.astype(jnp.float32))).astype(jnp.bfloat16)
    down_delta = (
        lax.dot_general(hidden, cotangent, (((0,), (0,)), ((), ())), preferred_element_type=jnp.float32)
        / math.sqrt(FW)
    ).astype(jnp.bfloat16)
    down_got = lax.all_to_all(down_delta, "path", split_axis=0, concat_axis=0, tiled=True)
    hidden_grad = lax.dot_general(
        cotangent, down_rows, (((1,), (2,)), ((), ())), preferred_element_type=jnp.float32
    ) / math.sqrt(FW)
    gate_grad = (
        hidden_grad * up_proj * sigmoid_gate * (1.0 + gate_pre * (1.0 - sigmoid_gate))
    ).astype(jnp.bfloat16)
    up_grad = (hidden_grad * activated).astype(jnp.bfloat16)
    grads = jnp.stack([gate_grad, up_grad], axis=2)
    gu_delta = (
        lax.dot_general(grads, normed, (((0,), (0,)), ((), ())), preferred_element_type=jnp.float32)
        / math.sqrt(D)
    ).astype(jnp.bfloat16)
    gu_got = lax.all_to_all(gu_delta, "path", split_axis=0, concat_axis=0, tiled=True)
    member = (path_module[:, None] == jnp.arange(module_count, dtype=jnp.int32)[None, :]).astype(
        jnp.int32
    ) * path_alive[:, None]
    weighting = member.astype(jnp.bfloat16)
    counts = jnp.sum(member, axis=0).astype(jnp.float32)
    contract_first = (((0,), (0,)), ((), ()))
    down_sum = lax.dot_general(
        weighting, down_got.reshape(path_count, -1), contract_first, preferred_element_type=jnp.float32
    ).reshape(module_count, 1, block_rows, width)
    gu_sum = lax.dot_general(
        weighting, gu_got.reshape(path_count, -1), contract_first, preferred_element_type=jnp.float32
    ).reshape(module_count, 2, block_rows, width)
    summed = jnp.concatenate([gu_sum, down_sum], axis=1)
    mean_delta = summed / counts[:, None, None, None]
    new_momentum = 0.9 * momentum + mean_delta
    new_params = (params.astype(jnp.float32) - 0.7 * (mean_delta + 0.9 * new_momentum)).astype(
        jnp.bfloat16
    )
    return (new_params, new_momentum)


def solution(mesh):
    return jax.shard_map(
        per_device,
        mesh=mesh,
        in_specs=(
            P(("path", "tensor"), None),
            P("path", None),
            P(None, None, ("tensor", "path"), None),
            P(None, None, ("tensor", "path"), None),
            P(),
            P(),
        ),
        out_specs=(
            P(None, None, ("tensor", "path"), None),
            P(None, None, ("tensor", "path"), None),
        ),
        check_vma=False,
    )
```

time: 452 us -> 416 us (0.920)
  the two profiles are of different devices: /device:TPU:8 before, /device:TPU:1 now
where the time goes in v3:
time: 416 us
  waiting for transfers between devices  286 us (69%)
  local copies, waits for them, and re-layouts  43.6 us (10%)
  starting transfers between devices  33.5 us (8%)
  matrix products  28.3 us (7%)
  between operations  14.2 us (3%)
  other arithmetic  10.2 us (2%)
    psum x1, waiting for transfers between devices, per_device(): output = lax.psum(partial_out, 'tensor')  150 us
    all_to_all x1, waiting for transfers between devices, per_device(): lax.all_to_all(picked, 'path', split_axis=0, concat_axis=0, tiled=True)  76.3 us
    all_to_all x1, waiting for transfers between devices, per_device(): lax.all_to_all(gu_delta, 'path', split_axis=0, concat_axis=0, tiled=True)  43.6 us
    all_to_all x1, starting transfers between devices, per_device(): lax.all_to_all(down_delta, 'path', split_axis=0, concat_axis=0, tiled=True)  16.8 us
    all_to_all x1, waiting for transfers between devices, per_device(): lax.all_to_all(down_delta, 'path', split_axis=0, concat_axis=0, tiled=True)  16 us
    all_to_all x1, starting transfers between devices, per_device(): lax.all_to_all(picked, 'path', split_axis=0, concat_axis=0, tiled=True)  11.5 us
  transfers between devices with their start and end apart: 5, of which 4 were waited for; matrix products, arithmetic and copies ran while one was open for 6% of the time, Pallas kernels for 0%

profile of v3, /device:TPU:1, one launch (start us, length us, event | category | flops | bytes accessed | tf_op | source)
XLA Modules:
  0.0 415.5 jit_solution(1962616376223606138)
XLA Ops:
  7.2 0.7 compare_select_fusion
  7.8 0.7 compare_and_fusion
  8.5 4.7 %gather_fusion = bf16[32,3,14,2048]{3,2,1,0:T(8,128)(2,1)} fusion(bf16[3,3,14,2048]{3,2,1,0:T(8,128)(2,1)} %param.8, s32[1024]{0:T(1024)S(1)} %pad_clamp_fusion), kind=kCustom, calls=%fused_computation | custom fusion | bytes 11010176 | tf_op jit(solution)/shard_map/jit(_take)/gather | solution.py:17
  13.1 6.1 %broadcast_select_fusion = bf16[32,3,14,2048]{3,2,1,0:T(8,128)(2,1)} fusion(bf16[32,3,14,2048]{3,2,1,0:T(8,128)(2,1)} %gather_fusion, pred[32]{0:T(512)(128)(4,1)S(1)} %compare_and_fusion), kind=kLoop, calls=%fused_computation.2 | loop fusion | flops 2752512 | bytes 11010080 | tf_op jit(solution)/shard_map/jit(_take)/select_n | solution.py:17
  19.2 11.5 %all-to-all-start = ((bf16[32,3,14,2048]{3,2,1,0:T(8,128)(2,1)}), bf16[32,3,14,2048]{3,2,1,0:T(8,128)(2,1)}, u32[]{:S(2)}, u32[]{:S(2)}) async-start(bf16[32,3,14,2048]{3,2,1,0:T(8,128)(2,1)} %broadcast_select_fusion), calls=%async_computation | async-start | bytes 12582912 | tf_op jit(solution)/shard_map/all_to_all | solution.py:18
  30.8 0.1 fusion.25
  30.9 0.7 fusion.26
  31.7 0.0 all-reduce.2.cloned.1.call-start
  31.7 76.3 %all-to-all-done = bf16[32,3,14,2048]{3,2,1,0:T(8,128)(2,1)} async-done(((bf16[32,3,14,2048]{3,2,1,0:T(8,128)(2,1)}), bf16[32,3,14,2048]{3,2,1,0:T(8,128)(2,1)}, u32[]{:S(2)}, u32[]{:S(2)}) %all-to-all-start) | async-done | bytes 5505056 | tf_op jit(solution)/shard_map/all_to_all | solution.py:18
  108.0 8.2 %copy.32 = bf16[32,3,14,2048]{3,0,2,1:T(8,128)(2,1)} copy(bf16[32,3,14,2048]{3,2,1,0:T(8,128)(2,1)} %all-to-all-done) | data formatting | bytes 11010048 | tf_op jit(solution)/shard_map/all_to_all | solution.py:18
  116.3 5.5 %convolution_multiply_fusion = f32[384,32,3,14]{0,1,3,2:T(8,128)S(1)} fusion(bf16[32,3,14,2048]{3,0,2,1:T(8,128)(2,1)} %copy.32, bf16[384,2048]{1,0:T(8,128)(2,1)} %all-gather.2.cloned.1.call-done), kind=kOutput, calls=%fused_computation.13 | convolution fusion | flops 2114445312 | bytes 9142272 | tf_op jit(solution)/shard_map/dot_general | solution.py:23
  121.8 1.4 copy-done.7
  123.2 4.2 %bitcast_multiply_fusion = f32[384,2048]{1,0:T(8,128)} fusion(bf16[32,3,14,2048]{3,0,2,1:T(8,128)(2,1)} %copy.32, f32[384,32,3,14]{0,1,3,2:T(8,128)S(1)} %convolution_multiply_fusion), kind=kOutput, calls=%fused_computation.6 | convolution fusion | flops 706461696 | bytes 6356992 | tf_op jit(solution)/shard_map/dot_general | solution.py:32
  127.5 149.8 %all-reduce.2.cloned.1.call-done = f32[384,2048]{1,0:T(8,128)} async-done(((f32[384,2048]{1,0:T(8,128)}), f32[384,2048]{1,0:T(8,128)}) %all-reduce.2.cloned.1.call-update) | async-done | bytes 3145744 | tf_op jit(solution)/shard_map/psum | solution.py:35
  277.3 3.5 multiply_convert_fusion.1
  280.8 2.4 copy.37
  283.1 16.8 %all-to-all-start.2 = ((bf16[32,14,2048]{2,1,0:T(8,128)(2,1)}), bf16[32,14,2048]{2,1,0:T(8,128)(2,1)S(1)}, u32[]{:S(2)}, u32[]{:S(2)}) async-start(bf16[32,14,2048]{2,1,0:T(8,128)(2,1)} %copy.37), calls=%async_computation.2 | async-start | bytes 4194304 | tf_op jit(solution)/shard_map/all_to_all | solution.py:41
  299.9 4.7 %fusion.24 = (bf16[384,32,1,14]{0,1,3,2:T(8,128)(2,1)S(1)}, bf16[384,32,1,14]{0,1,3,2:T(8,128)(2,1)S(1)}) fusion(f32[384,32,3,14]{0,1,3,2:T(8,128)} %copy-done.7, bf16[32,3,14,2048]{3,0,2,1:T(8,128)(2,1)} %copy.32, f32[384,2048]{1,0:T(8,128)} %all-reduce.2.cloned.1.call-done, bf16[384,2048]{1,0:T(8,128)(2,1)} %param.7), kind=kOutput, calls=%fused_computation.42 | convolution fusion | flops 710197248 | bytes 8617984 | tf_op jit(solution)/shard_map/dot_general | solution.py:42
  304.6 2.1 multiply_convert_fusion
  306.7 5.6 %copy.34 = bf16[32,2,14,2048]{3,1,2,0:T(2,128)(2,1)} copy(bf16[32,2,14,2048]{3,0,2,1:T(8,128)(2,1)S(1)} %multiply_convert_fusion) | data formatting | bytes 7340032 | tf_op jit(solution)/shard_map/convert_element_type | solution.py:53
  312.3 16.0 %all-to-all-done.2 = bf16[32,14,2048]{2,1,0:T(8,128)(2,1)S(1)} async-done(((bf16[32,14,2048]{2,1,0:T(8,128)(2,1)}), bf16[32,14,2048]{2,1,0:T(8,128)(2,1)S(1)}, u32[]{:S(2)}, u32[]{:S(2)}) %all-to-all-start.2) | async-done | bytes 1835040 | tf_op jit(solution)/shard_map/all_to_all | solution.py:41
  328.2 5.2 %all-to-all-start.1 = ((bf16[32,2,14,2048]{3,1,2,0:T(2,128)(2,1)}), bf16[32,2,14,2048]{3,1,2,0:T(2,128)(2,1)}, u32[]{:S(2)}, u32[]{:S(2)}) async-start(bf16[32,2,14,2048]{3,1,2,0:T(2,128)(2,1)} %copy.34), calls=%async_computation.1 | async-start | bytes 7340032 | tf_op jit(solution)/shard_map/all_to_all | solution.py:54
  333.5 0.1 select_reduce_fusion
  333.6 2.0 convolution_bitcast_fusion
  335.7 43.6 %all-to-all-done.1 = bf16[32,2,14,2048]{3,1,2,0:T(2,128)(2,1)} async-done(((bf16[32,2,14,2048]{3,1,2,0:T(2,128)(2,1)}), bf16[32,2,14,2048]{3,1,2,0:T(2,128)(2,1)}, u32[]{:S(2)}, u32[]{:S(2)}) %all-to-all-start.1) | async-done | bytes 3670048 | tf_op jit(solution)/shard_map/all_to_all | solution.py:54
  379.3 5.8 %copy.35 = bf16[32,2,14,2048]{3,2,1,0:T(8,128)(2,1)} copy(bf16[32,2,14,2048]{3,1,2,0:T(2,128)(2,1)} %all-to-all-done.1) | data formatting | bytes 7340032 | tf_op jit(solution)/shard_map/all_to_all | solution.py:54
  385.1 6.4 %reshape.38 = bf16[32,57344]{1,0:T(8,128)(2,1)} reshape(bf16[32,2,14,2048]{3,2,1,0:T(8,128)(2,1)} %copy.35) | data formatting | bytes 7340032 | tf_op jit(solution)/shard_map/reshape | solution.py:65
  391.4 6.4 %dot_general.34 = bf16[2,14,2048,32]{2,1,0,3:T(8,128)(2,1)} reshape(bf16[57344,32]{0,1:T(8,128)(2,1)} %bitcast.94) | data formatting | bytes 7340032 | tf_op jit(solution)/shard_map/dot_general | solution.py:64
  397.8 6.3 %fusion = f32[3,2,14,2048]{3,0,2,1:T(4,128)S(1)} fusion(bf16[2,14,2048,32]{2,1,0,3:T(8,128)(2,1)} %dot_general.34, s32[32]{0:T(128)S(1)} %copy-done.3, s32[32]{0:T(128)S(1)} %copy-done.4), kind=kOutput, calls=%fused_computation.3 | convolution fusion | flops 11010336 | bytes 4358400 | tf_op jit(solution)/shard_map/dot_general | solution.py:64
  404.1 1.7 fusion.8
  405.9 1.6 copy.41
  407.5 1.2 copy.40
  (22 shorter events, 0.1 us)
Async XLA Ops:
  19.2 11.5 %copy-start.2 = (bf16[24,2048]{1,0:T(8,128)(2,1)S(1)}, bf16[24,2048]{1,0:T(8,128)(2,1)}, u32[]{:S(2)}) copy-start(bf16[24,2048]{1,0:T(8,128)(2,1)} %param.6) | copy-start | bytes 294916
  19.2 88.8 %all-to-all-start = ((bf16[32,3,14,2048]{3,2,1,0:T(8,128)(2,1)}), bf16[32,3,14,2048]{3,2,1,0:T(8,128)(2,1)}, u32[]{:S(2)}, u32[]{:S(2)}) async-start(bf16[32,3,14,2048]{3,2,1,0:T(8,128)(2,1)} %broadcast_select_fusion), calls=%async_computation | async-start | bytes 12582912 | tf_op jit(solution)/shard_map/all_to_all | solution.py:18
  30.7 85.6 %all-gather.2.cloned.1.call-start = ((), (), s32[]{:S(2)}) async-start(), calls=%async_computation.3 | async-start | bytes 1671168 | tf_op jit(solution)/shard_map/all_gather | solution.py:22
  31.7 245.6 %all-reduce.2.cloned.1.call-start = ((), (), s32[]{:S(2)}) async-start(), calls=%async_computation.4 | async-start | bytes 6291456 | tf_op jit(solution)/shard_map/psum | solution.py:35
  121.8 1.4 copy-start.7
  127.4 149.8 %copy-start.5 = (bf16[384,2048]{1,0:T(8,128)(2,1)S(1)}, bf16[384,2048]{1,0:T(8,128)(2,1)}, u32[]{:S(2)}) copy-start(bf16[384,2048]{1,0:T(8,128)(2,1)} %param.7) | copy-start | bytes 4718596
  283.1 45.1 %all-to-all-start.2 = ((bf16[32,14,2048]{2,1,0:T(8,128)(2,1)}), bf16[32,14,2048]{2,1,0:T(8,128)(2,1)S(1)}, u32[]{:S(2)}, u32[]{:S(2)}) async-start(bf16[32,14,2048]{2,1,0:T(8,128)(2,1)} %copy.37), calls=%async_computation.2 | async-start | bytes 4194304 | tf_op jit(solution)/shard_map/all_to_all | solution.py:41
  299.9 4.7 %copy-start.6 = (bf16[384,2048]{1,0:T(8,128)(2,1)S(1)}, bf16[384,2048]{1,0:T(8,128)(2,1)}, u32[]{:S(2)}) copy-start(bf16[384,2048]{1,0:T(8,128)(2,1)} %all-gather.2.cloned.1.call-done) | copy-start | bytes 4718596
  312.3 21.2 %copy-start.3 = (s32[32]{0:T(128)S(1)}, s32[32]{0:T(128)}, u32[]{:S(2)}) copy-start(s32[32]{0:T(128)} %param.10) | copy-start | bytes 388
  312.3 21.2 %copy-start.4 = (s32[32]{0:T(128)S(1)}, s32[32]{0:T(128)}, u32[]{:S(2)}) copy-start(s32[32]{0:T(128)} %param.11) | copy-start | bytes 388
  328.2 51.0 %all-to-all-start.1 = ((bf16[32,2,14,2048]{3,1,2,0:T(2,128)(2,1)}), bf16[32,2,14,2048]{3,1,2,0:T(2,128)(2,1)}, u32[]{:S(2)}, u32[]{:S(2)}) async-start(bf16[32,2,14,2048]{3,1,2,0:T(2,128)(2,1)} %copy.34), calls=%async_computation.1 | async-start | bytes 7340032 | tf_op jit(solution)/shard_map/all_to_all | solution.py:54
  397.8 6.3 %copy-start = (bf16[3,3,14,2048]{3,2,1,0:T(8,128)(2,1)S(1)}, bf16[3,3,14,2048]{3,2,1,0:T(8,128)(2,1)}, u32[]{:S(2)}) copy-start(bf16[3,3,14,2048]{3,2,1,0:T(8,128)(2,1)} %param.8) | copy-start | bytes 1548292
  397.8 6.3 %copy-start.1 = (f32[3,3,14,2048]{3,2,1,0:T(8,128)S(1)}, f32[3,3,14,2048]{3,2,1,0:T(8,128)}, u32[]{:S(2)}) copy-start(f32[3,3,14,2048]{3,2,1,0:T(8,128)} %param.9) | copy-start | bytes 3096580
Sparse Core Ops, SparseCore 0:
  34.2 64.7 all-gather.1
  127.6 149.6 all-reduce.1

commit v4 on v1

--- a/solution.py
+++ b/solution.py
@@ -16,10 +16,10 @@
     path_count = path_alive.shape[0]
     contract_last = (((1,), (1,)), ((), ()))
     contract_first = (((0,), (0,)), ((), ()))
-    picked = jnp.take(params, path_module, axis=0)
-    rows = lax.all_to_all(picked, "path", split_axis=0, concat_axis=0, tiled=True)
+    picked = jnp.transpose(jnp.take(params, path_module, axis=0), (1, 2, 0, 3))
+    rows = lax.all_to_all(picked, "path", split_axis=2, concat_axis=2, tiled=True)
     local_rows = path_count * block_rows
-    rows = jnp.moveaxis(rows, 1, 0).reshape(3, local_rows, width)
+    rows = rows.reshape(3, local_rows, width)
     gate_rows, up_rows, down_rows = rows[0], rows[1], rows[2]
     own = hidden_in.astype(jnp.float32)
     mean_sq = jnp.mean(jnp.square(own), axis=1, keepdims=True)
@@ -35,16 +35,20 @@
     activated = gate_pre * sigmoid_gate
     hidden = (activated * up_proj).astype(jnp.bfloat16)
     partial_out = jnp.dot(hidden, down_rows, preferred_element_type=jnp.float32) / math.sqrt(FW)
-    out_rows = lax.psum_scatter(partial_out, "tensor", scatter_dimension=0, tiled=True)
-    own_count = out_rows.shape[0]
-    start = lax.axis_index("tensor") * own_count
-    target = lax.dynamic_slice_in_dim(teacher, start, own_count, 0)
-    own_cot = (4.0 * (out_rows - target.astype(jnp.float32))).astype(jnp.bfloat16)
-    cotangent = lax.all_gather(own_cot, "tensor", axis=0, tiled=True)
+    output = lax.psum(partial_out, "tensor")
+    cotangent = (4.0 * (output - teacher.astype(jnp.float32))).astype(jnp.bfloat16)
+    piece_shape = (block_rows, path_count, width)
+
+    def send_back(delta):
+        return lax.all_to_all(
+            delta.reshape(piece_shape), "path", split_axis=1, concat_axis=1, tiled=True
+        )
+
     down_delta = (
         lax.dot_general(hidden, cotangent, contract_first, preferred_element_type=jnp.float32)
         / math.sqrt(FW)
     ).astype(jnp.bfloat16)
+    down_got = send_back(down_delta)
     hidden_grad = lax.dot_general(
         cotangent, down_rows, contract_last, preferred_element_type=jnp.float32
     ) / math.sqrt(FW)
@@ -56,23 +60,22 @@
         lax.dot_general(gate_grad, normed, contract_first, preferred_element_type=jnp.float32)
         / math.sqrt(D)
     ).astype(jnp.bfloat16)
+    gate_got = send_back(gate_delta)
     up_delta = (
         lax.dot_general(up_grad, normed, contract_first, preferred_element_type=jnp.float32)
         / math.sqrt(D)
     ).astype(jnp.bfloat16)
+    up_got = send_back(up_delta)
     member = (path_module[:, None] == jnp.arange(module_count, dtype=jnp.int32)[None, :]).astype(
         jnp.int32
     ) * path_alive[:, None]
-    weighting = member.astype(jnp.bfloat16)
     counts = jnp.sum(member, axis=0).astype(jnp.float32)
-    deltas = jnp.stack([gate_delta, up_delta, down_delta]).reshape(3, path_count, block_rows, width)
-    got = lax.all_to_all(
-        jnp.moveaxis(deltas, 1, 0), "path", split_axis=0, concat_axis=0, tiled=True
-    )
-    summed = lax.dot_general(
-        weighting, got.reshape(path_count, -1), contract_first, preferred_element_type=jnp.float32
-    )
-    summed = summed.reshape(module_count, 3, block_rows, width)
+    weights_t = member.T.astype(jnp.float32)
+
+    def module_sums(got):
+        return jnp.sum(got.astype(jnp.float32)[None] * weights_t[:, None, :, None], axis=2)
+
+    summed = jnp.stack([module_sums(gate_got), module_sums(up_got), module_sums(down_got)], axis=1)
     mean_delta = summed / counts[:, None, None, None]
     new_momentum = 0.9 * momentum + mean_delta
     new_params = (params.astype(jnp.float32) - 0.7 * (mean_delta + 0.9 * new_momentum)).astype(

time: 452 us -> 416 us (0.920)
  the two profiles are of different devices: /device:TPU:8 before, /device:TPU:1 now
where the time goes in v4:
time: 416 us
  waiting for transfers between devices  294 us (71%)
  starting transfers between devices  38.2 us (9%)
  other arithmetic  27.7 us (7%)
  local copies, waits for them, and re-layouts  24 us (6%)
  matrix products  17.5 us (4%)
  between operations  14.3 us (3%)
    psum x1, waiting for transfers between devices, per_device(): output = lax.psum(partial_out, 'tensor')  150 us
    all_to_all x1, waiting for transfers between devices, per_device(): lax.all_to_all(picked, 'path', split_axis=2, concat_axis=2, tiled=True)  76.3 us
    all_to_all x3, waiting for transfers between devices, send_back(): lax.all_to_all(delta.reshape(piece_shape), 'path', split_axis=1, concat_a...  67.8 us
    all_to_all x3, starting transfers between devices, send_back(): lax.all_to_all(delta.reshape(piece_shape), 'path', split_axis=1, concat_a...  26.7 us
    all_to_all x1, starting transfers between devices, per_device(): lax.all_to_all(picked, 'path', split_axis=2, concat_axis=2, tiled=True)  11.5 us
    convert_element_type x3, other arithmetic, module_sums(): got.astype(jnp.float32)[None] * weights_t[:, None, :, None]  10.2 us
    slice x4, local copies, waits for them, and re-layouts, per_device(): gate_rows, up_rows, down_rows = (rows[0], rows[1], rows[2])  9.49 us
    reduce_sum x1, other arithmetic, module_sums(): jnp.sum(got.astype(jnp.float32)[None] * weights_t[:, None, :, None], axis=2)  8.68 us
  transfers between devices with their start and end apart: 6, of which 5 were waited for; matrix products, arithmetic and copies ran while one was open for 7% of the time, Pallas kernels for 0%

profile of v4, /device:TPU:1, one launch (start us, length us, event | category | flops | bytes accessed | tf_op | source)
XLA Modules:
  0.0 415.8 jit_solution(4861789979527981877)
XLA Ops:
  8.5 4.6 %gather_fusion = bf16[32,3,14,2048]{3,2,1,0:T(8,128)(2,1)} fusion(bf16[3,3,14,2048]{3,2,1,0:T(8,128)(2,1)} %param.8, s32[1024]{0:T(1024)S(1)} %pad_clamp_fusion), kind=kCustom, calls=%fused_computation | custom fusion | bytes 11010176 | tf_op jit(solution)/shard_map/jit(_take)/gather | solution.py:19
  13.1 6.1 %select_bitcast_fusion = bf16[3,14,32,2048]{3,1,0,2:T(8,128)(2,1)} fusion(bf16[32,3,14,2048]{3,2,1,0:T(8,128)(2,1)} %gather_fusion, pred[32]{0:T(512)(128)(4,1)S(1)} %compare_and_fusion), kind=kLoop, calls=%fused_computation.4 | loop fusion | flops 2752512 | bytes 11010080 | tf_op jit(solution)/shard_map/jit(_take)/select_n | solution.py:19
  19.2 11.5 %all-to-all-start = ((bf16[3,14,32,2048]{3,1,0,2:T(8,128)(2,1)}), bf16[3,14,32,2048]{3,1,0,2:T(8,128)(2,1)}, u32[]{:S(2)}, u32[]{:S(2)}) async-start(bf16[3,14,32,2048]{3,1,0,2:T(8,128)(2,1)} %select_bitcast_fusion), calls=%async_computation | async-start | bytes 12582912 | tf_op jit(solution)/shard_map/all_to_all | solution.py:20
  30.9 0.7 fusion.4
  31.7 76.3 %all-to-all-done = bf16[3,14,32,2048]{3,1,0,2:T(8,128)(2,1)} async-done(((bf16[3,14,32,2048]{3,1,0,2:T(8,128)(2,1)}), bf16[3,14,32,2048]{3,1,0,2:T(8,128)(2,1)}, u32[]{:S(2)}, u32[]{:S(2)}) %all-to-all-start) | async-done | bytes 5505056 | tf_op jit(solution)/shard_map/all_to_all | solution.py:20
  108.0 4.0 fusion.8
  112.0 2.3 copy.34
  114.3 2.2 copy.35
  116.5 1.0 copy.36
  117.5 3.3 convolution_multiply_fusion.3
  120.8 2.0 multiply_convert_fusion.6
  123.6 2.7 convolution_multiply_fusion
  126.3 149.8 %all-reduce.2.cloned.1.call-done = f32[384,2048]{1,0:T(8,128)} async-done(((f32[384,2048]{1,0:T(8,128)}), f32[384,2048]{1,0:T(8,128)}) %all-reduce.2.cloned.1.call-update) | async-done | bytes 3145744 | tf_op jit(solution)/shard_map/psum | solution.py:38
  276.2 3.2 convolution_multiply_fusion.1
  279.4 1.3 multiply_convert_fusion.2
  280.7 2.3 copy.37
  283.0 17.1 %all-to-all-start.1 = ((bf16[14,32,2048]{2,0,1:T(8,128)(2,1)}), bf16[14,32,2048]{2,0,1:T(8,128)(2,1)}, u32[]{:S(2)}, u32[]{:S(2)}) async-start(bf16[14,32,2048]{2,0,1:T(8,128)(2,1)} %copy.37), calls=%async_computation.1 | async-start | bytes 4194304 | tf_op jit(solution)/shard_map/all_to_all | solution.py:43
  300.1 2.6 multiply_convert_fusion
  302.7 2.4 copy.41
  305.0 23.4 %all-to-all-done.1 = bf16[14,32,2048]{2,0,1:T(8,128)(2,1)} async-done(((bf16[14,32,2048]{2,0,1:T(8,128)(2,1)}), bf16[14,32,2048]{2,0,1:T(8,128)(2,1)}, u32[]{:S(2)}, u32[]{:S(2)}) %all-to-all-start.1) | async-done | bytes 1835040 | tf_op jit(solution)/shard_map/all_to_all | solution.py:43
  328.5 4.5 %all-to-all-start.3 = ((bf16[14,32,2048]{2,0,1:T(8,128)(2,1)}), bf16[14,32,2048]{2,0,1:T(8,128)(2,1)S(1)}, u32[]{:S(2)}, u32[]{:S(2)}) async-start(bf16[14,32,2048]{2,0,1:T(8,128)(2,1)} %copy.41), calls=%async_computation.3 | async-start | bytes 4194304 | tf_op jit(solution)/shard_map/all_to_all | solution.py:43
  333.0 2.6 multiply_convert_fusion.1
  335.5 2.4 copy.39
  338.0 23.4 %all-to-all-done.3 = bf16[14,32,2048]{2,0,1:T(8,128)(2,1)S(1)} async-done(((bf16[14,32,2048]{2,0,1:T(8,128)(2,1)}), bf16[14,32,2048]{2,0,1:T(8,128)(2,1)S(1)}, u32[]{:S(2)}, u32[]{:S(2)}) %all-to-all-start.3) | async-done | bytes 1835040 | tf_op jit(solution)/shard_map/all_to_all | solution.py:43
  361.4 5.2 %all-to-all-start.2 = ((bf16[14,32,2048]{2,0,1:T(8,128)(2,1)}), bf16[14,32,2048]{2,0,1:T(8,128)(2,1)}, u32[]{:S(2)}, u32[]{:S(2)}) async-start(bf16[14,32,2048]{2,0,1:T(8,128)(2,1)} %copy.39), calls=%async_computation.2 | async-start | bytes 4194304 | tf_op jit(solution)/shard_map/all_to_all | solution.py:43
  366.7 4.4 %copy_convert_fusion.2 = f32[14,32,2048]{2,1,0:T(8,128)} fusion(bf16[14,32,2048]{2,0,1:T(8,128)(2,1)} %all-to-all-done.1), kind=kLoop, calls=%fused_computation.12 | loop fusion | flops 917504 | bytes 5505024 | tf_op jit(solution)/shard_map/convert_element_type | solution.py:76
  371.1 2.9 copy_convert_fusion
  374.1 21.0 %all-to-all-done.2 = bf16[14,32,2048]{2,0,1:T(8,128)(2,1)} async-done(((bf16[14,32,2048]{2,0,1:T(8,128)(2,1)}), bf16[14,32,2048]{2,0,1:T(8,128)(2,1)}, u32[]{:S(2)}, u32[]{:S(2)}) %all-to-all-start.2) | async-done | bytes 1835040 | tf_op jit(solution)/shard_map/all_to_all | solution.py:43
  395.0 2.8 copy_convert_fusion.1
  397.9 8.7 %multiply_reduce_fusion.2 = (f32[3,14,2048]{2,1,0:T(8,128)S(1)}, f32[3,14,2048]{2,1,0:T(8,128)S(1)}, f32[3,14,2048]{2,1,0:T(8,128)S(1)}) fusion(f32[3,32]{1,0:T(4,128)S(1)} %select_convert_fusion, f32[14,32,2048]{2,1,0:T(8,128)S(1)} %copy-done.1, f32[14,32,2048]{2,1,0:T(8,128)S(1)} %copy_convert_fusion.1, f32[14,32,2048]{2,1,0:T(8,128)} %copy_convert_fusion), kind=kLoop, calls=%fused_computation.3 | loop fusion | flops 16257024 | bytes 12042624 | tf_op jit(solution)/shard_map/reduce_sum | solution.py:76
  407.0 1.1 copy.45
  408.1 0.9 copy.44
  (52 shorter events, 3.0 us)
Async XLA Ops:
  19.2 11.5 %copy-start.10 = (bf16[24,2048]{1,0:T(8,128)(2,1)S(1)}, bf16[24,2048]{1,0:T(8,128)(2,1)}, u32[]{:S(2)}) copy-start(bf16[24,2048]{1,0:T(8,128)(2,1)} %param.6) | copy-start | bytes 294916
  19.2 88.8 %all-to-all-start = ((bf16[3,14,32,2048]{3,1,0,2:T(8,128)(2,1)}), bf16[3,14,32,2048]{3,1,0,2:T(8,128)(2,1)}, u32[]{:S(2)}, u32[]{:S(2)}) async-start(bf16[3,14,32,2048]{3,1,0,2:T(8,128)(2,1)} %select_bitcast_fusion), calls=%async_computation | async-start | bytes 12582912 | tf_op jit(solution)/shard_map/all_to_all | solution.py:20
  30.7 86.9 %all-gather.2.cloned.1.call-start = ((), (), s32[]{:S(2)}) async-start(), calls=%async_computation.4 | async-start | bytes 1671168 | tf_op jit(solution)/shard_map/all_gather | solution.py:27
  31.6 244.5 %all-reduce.2.cloned.1.call-start = ((), (), s32[]{:S(2)}) async-start(), calls=%async_computation.5 | async-start | bytes 6291456 | tf_op jit(solution)/shard_map/psum | solution.py:38
  117.5 3.3 copy-start.6
  117.5 3.3 copy-start.13
  120.8 2.1 copy-start.15
  122.9 0.7 copy-start.4
  126.3 149.9 %copy-start.3 = (bf16[384,2048]{1,0:T(8,128)(2,1)S(1)}, bf16[384,2048]{1,0:T(8,128)(2,1)}, u32[]{:S(2)}) copy-start(bf16[384,2048]{1,0:T(8,128)(2,1)} %param.7) | copy-start | bytes 4718596
  276.2 3.2 copy-start.14
  276.2 3.2 copy-start.16
  276.2 3.2 copy-start.18
  279.4 1.3 copy-start.8
  283.0 17.1 %copy-start.2 = (f32[384,2048]{1,0:T(8,128)S(1)}, f32[384,2048]{1,0:T(8,128)}, u32[]{:S(2)}) copy-start(f32[384,2048]{1,0:T(8,128)} %all-reduce.2.cloned.1.call-done) | copy-start | bytes 9437188
  283.0 17.1 %copy-start.5 = (bf16[384,448]{0,1:T(8,128)(2,1)S(1)}, bf16[384,448]{0,1:T(8,128)(2,1)}, u32[]{:S(2)}) copy-start(bf16[384,448]{0,1:T(8,128)(2,1)} %copy-done.4) | copy-start | bytes 1032196
  283.0 45.5 %all-to-all-start.1 = ((bf16[14,32,2048]{2,0,1:T(8,128)(2,1)}), bf16[14,32,2048]{2,0,1:T(8,128)(2,1)}, u32[]{:S(2)}, u32[]{:S(2)}) async-start(bf16[14,32,2048]{2,0,1:T(8,128)(2,1)} %copy.37), calls=%async_computation.1 | async-start | bytes 4194304 | tf_op jit(solution)/shard_map/all_to_all | solution.py:43
  305.0 27.9 %copy-start.9 = (f32[384,448]{0,1:T(8,128)S(1)}, f32[384,448]{0,1:T(8,128)}, u32[]{:S(2)}) copy-start(f32[384,448]{0,1:T(8,128)} %copy-done.8) | copy-start | bytes 2064388
  305.0 28.0 %copy-start.17 = (f32[384,448]{0,1:T(8,128)S(1)}, f32[384,448]{0,1:T(8,128)}, u32[]{:S(2)}) copy-start(f32[384,448]{0,1:T(8,128)} %copy-done.15) | copy-start | bytes 2064388
  328.5 32.9 %all-to-all-start.3 = ((bf16[14,32,2048]{2,0,1:T(8,128)(2,1)}), bf16[14,32,2048]{2,0,1:T(8,128)(2,1)S(1)}, u32[]{:S(2)}, u32[]{:S(2)}) async-start(bf16[14,32,2048]{2,0,1:T(8,128)(2,1)} %copy.41), calls=%async_computation.3 | async-start | bytes 4194304 | tf_op jit(solution)/shard_map/all_to_all | solution.py:43
  338.0 28.6 %copy-start.11 = (s32[32]{0:T(128)S(1)}, s32[32]{0:T(128)}, u32[]{:S(2)}) copy-start(s32[32]{0:T(128)} %param.10) | copy-start | bytes 388
  338.0 28.6 %copy-start.12 = (s32[32]{0:T(128)S(1)}, s32[32]{0:T(128)}, u32[]{:S(2)}) copy-start(s32[32]{0:T(128)} %param.11) | copy-start | bytes 388
  361.4 33.6 %all-to-all-start.2 = ((bf16[14,32,2048]{2,0,1:T(8,128)(2,1)}), bf16[14,32,2048]{2,0,1:T(8,128)(2,1)}, u32[]{:S(2)}, u32[]{:S(2)}) async-start(bf16[14,32,2048]{2,0,1:T(8,128)(2,1)} %copy.39), calls=%async_computation.2 | async-start | bytes 4194304 | tf_op jit(solution)/shard_map/all_to_all | solution.py:43
  395.0 2.8 copy-start.1
  397.9 8.7 %copy-start = (bf16[3,3,14,2048]{3,2,1,0:T(8,128)(2,1)S(1)}, bf16[3,3,14,2048]{3,2,1,0:T(8,128)(2,1)}, u32[]{:S(2)}) copy-start(bf16[3,3,14,2048]{3,2,1,0:T(8,128)(2,1)} %param.8) | copy-start | bytes 1548292
  397.9 8.7 %copy-start.7 = (f32[3,3,14,2048]{3,2,1,0:T(8,128)S(1)}, f32[3,3,14,2048]{3,2,1,0:T(8,128)}, u32[]{:S(2)}) copy-start(f32[3,3,14,2048]{3,2,1,0:T(8,128)} %param.9) | copy-start | bytes 3096580
Sparse Core Ops, SparseCore 0:
  34.1 64.8 all-gather.1
  126.5 149.6 all-reduce.1

commit v5 on v4

--- a/solution.py
+++ b/solution.py
@@ -16,7 +16,7 @@
     path_count = path_alive.shape[0]
     contract_last = (((1,), (1,)), ((), ()))
     contract_first = (((0,), (0,)), ((), ()))
-    picked = jnp.transpose(jnp.take(params, path_module, axis=0), (1, 2, 0, 3))
+    picked = jnp.transpose(jnp.take(params, path_module, axis=0, mode="clip"), (1, 2, 0, 3))
     rows = lax.all_to_all(picked, "path", split_axis=2, concat_axis=2, tiled=True)
     local_rows = path_count * block_rows
     rows = rows.reshape(3, local_rows, width)
@@ -70,17 +70,25 @@
         jnp.int32
     ) * path_alive[:, None]
     counts = jnp.sum(member, axis=0).astype(jnp.float32)
-    weights_t = member.T.astype(jnp.float32)
-
-    def module_sums(got):
-        return jnp.sum(got.astype(jnp.float32)[None] * weights_t[:, None, :, None], axis=2)
-
-    summed = jnp.stack([module_sums(gate_got), module_sums(up_got), module_sums(down_got)], axis=1)
-    mean_delta = summed / counts[:, None, None, None]
-    new_momentum = 0.9 * momentum + mean_delta
-    new_params = (params.astype(jnp.float32) - 0.7 * (mean_delta + 0.9 * new_momentum)).astype(
-        jnp.bfloat16
-    )
+    new_momentum = []
+    new_params = []
+    weighting = member.astype(jnp.bfloat16)
+    for j, got in enumerate((gate_got, up_got, down_got)):
+        got, weighting_j, momentum_j, params_j = lax.optimization_barrier(
+            (got, weighting, momentum[:, j], params[:, j])
+        )
+        summed = lax.dot_general(
+            weighting_j, got, (((0,), (1,)), ((), ())), preferred_element_type=jnp.float32
+        )
+        mean_delta = summed / counts[:, None, None]
+        momentum_j = 0.9 * momentum_j + mean_delta
+        params_j = (params_j.astype(jnp.float32) - 0.7 * (mean_delta + 0.9 * momentum_j)).astype(
+            jnp.bfloat16
+        )
+        new_momentum.append(momentum_j)
+        new_params.append(params_j)
+    new_momentum = jnp.stack(new_momentum, axis=1)
+    new_params = jnp.stack(new_params, axis=1)
     return (new_params, new_momentum)
 
 

time: 416 us -> 410 us (0.986)
  other arithmetic: 27.7 us -> 2.83 us
  matrix products: 17.5 us -> 27.3 us
  local copies, waits for them, and re-layouts: 24 us -> 29 us
    convert_element_type x4 -> x0, other arithmetic: 10.2 us -> none  [the longest x3 10.2 us: module_sums(): got.astype(jnp.float32)[None] * weights_t[:, None, :, None]]
    dot_general x0 -> x3, matrix products: none -> 10.1 us  [per_device(): lax.dot_general(weighting_j, got, (((0,), (1,)), ((), ())), preferred_ele...]
    reduce_sum x1 -> x0, other arithmetic: 8.68 us -> none  [module_sums(): jnp.sum(got.astype(jnp.float32)[None] * weights_t[:, None, :, None], axis=2)]
    select_n x2 -> x0, other arithmetic: 6.73 us -> none  [per_device(): picked = jnp.transpose(jnp.take(params, path_module, axis=0), (1, 2, 0, 3))]
    unnamed x40 -> x50, local copies, waits for them, and re-layouts: 2.75 us -> 7.57 us
  transfers between devices with their start and end apart: 6 -> 6, of which waited for: 5 -> 5; matrix products, arithmetic and copies ran while one was open for 7% -> 6% of each run, Pallas kernels for 0% -> 0%
where the time goes in v5:
time: 410 us; the launch traced here: 409 us
  waiting for transfers between devices  297 us (72%)
  starting transfers between devices  38.2 us (9%)
  local copies, waits for them, and re-layouts  29 us (7%)
  matrix products  27.3 us (7%)
  between operations  14.4 us (4%)
    psum x1, waiting for transfers between devices, per_device(): output = lax.psum(partial_out, 'tensor')  150 us
    all_to_all x1, waiting for transfers between devices, per_device(): lax.all_to_all(picked, 'path', split_axis=2, concat_axis=2, tiled=True)  76.3 us
    all_to_all x3, waiting for transfers between devices, send_back(): lax.all_to_all(delta.reshape(piece_shape), 'path', split_axis=1, concat_a...  71.2 us
    all_to_all x3, starting transfers between devices, send_back(): lax.all_to_all(delta.reshape(piece_shape), 'path', split_axis=1, concat_a...  26.7 us
    all_to_all x1, starting transfers between devices, per_device(): lax.all_to_all(picked, 'path', split_axis=2, concat_axis=2, tiled=True)  11.5 us
    dot_general x3, matrix products, per_device(): lax.dot_general(weighting_j, got, (((0,), (1,)), ((), ())), preferred_ele...  10.1 us
    slice x4, local copies, waits for them, and re-layouts, per_device(): gate_rows, up_rows, down_rows = (rows[0], rows[1], rows[2])  9.49 us
  transfers between devices with their start and end apart: 6, of which 5 were waited for; matrix products, arithmetic and copies ran while one was open for 6% of the time, Pallas kernels for 0%

profile of v5, /device:TPU:1, one launch (start us, length us, event | category | flops | bytes accessed | tf_op | source)
XLA Modules:
  0.0 409.1 jit_solution(1168579440316608955)
XLA Ops:
  7.8 4.6 %gather_fusion = bf16[32,3,14,2048]{3,2,1,0:T(8,128)(2,1)} fusion(bf16[3,3,14,2048]{3,2,1,0:T(8,128)(2,1)} %param.8, s32[1024]{0:T(1024)S(1)} %pad_clamp_fusion), kind=kCustom, calls=%fused_computation | custom fusion | bytes 11010176 | tf_op jit(solution)/shard_map/jit(_take)/gather | solution.py:19
  12.5 11.5 %all-to-all-start = ((bf16[3,14,32,2048]{3,1,0,2:T(8,128)(2,1)}), bf16[3,14,32,2048]{3,1,0,2:T(8,128)(2,1)}, u32[]{:S(2)}, u32[]{:S(2)}) async-start(bf16[3,14,32,2048]{3,1,0,2:T(8,128)(2,1)} %bitcast.60), calls=%async_computation | async-start | bytes 12582912 | tf_op jit(solution)/shard_map/all_to_all | solution.py:20
  24.9 76.3 %all-to-all-done = bf16[3,14,32,2048]{3,1,0,2:T(8,128)(2,1)} async-done(((bf16[3,14,32,2048]{3,1,0,2:T(8,128)(2,1)}), bf16[3,14,32,2048]{3,1,0,2:T(8,128)(2,1)}, u32[]{:S(2)}, u32[]{:S(2)}) %all-to-all-start) | async-done | bytes 5505056 | tf_op jit(solution)/shard_map/all_to_all | solution.py:20
  101.3 4.0 fusion.19
  105.3 2.2 copy.35
  107.5 2.3 copy.36
  109.8 1.0 copy.37
  110.8 3.3 convolution_multiply_fusion.3
  114.1 2.0 multiply_convert_fusion.6
  116.8 2.7 convolution_multiply_fusion
  119.6 149.8 %all-reduce.2.cloned.1.call-done = f32[384,2048]{1,0:T(8,128)} async-done(((f32[384,2048]{1,0:T(8,128)}), f32[384,2048]{1,0:T(8,128)}) %all-reduce.2.cloned.1.call-update) | async-done | bytes 3145744 | tf_op jit(solution)/shard_map/psum | solution.py:38
  269.4 3.2 convolution_multiply_fusion.1
  272.6 1.1 multiply_convert_fusion.1
  273.8 2.3 copy.42
  276.2 17.1 %all-to-all-start.2 = ((bf16[14,32,2048]{2,0,1:T(8,128)(2,1)}), bf16[14,32,2048]{2,0,1:T(8,128)(2,1)}, u32[]{:S(2)}, u32[]{:S(2)}) async-start(bf16[14,32,2048]{2,0,1:T(8,128)(2,1)} %copy.42), calls=%async_computation.2 | async-start | bytes 4194304 | tf_op jit(solution)/shard_map/all_to_all | solution.py:43
  293.3 2.4 multiply_convert_fusion.2
  295.6 2.4 copy.38
  298.1 23.6 %all-to-all-done.2 = bf16[14,32,2048]{2,0,1:T(8,128)(2,1)} async-done(((bf16[14,32,2048]{2,0,1:T(8,128)(2,1)}), bf16[14,32,2048]{2,0,1:T(8,128)(2,1)}, u32[]{:S(2)}, u32[]{:S(2)}) %all-to-all-start.2) | async-done | bytes 1835040 | tf_op jit(solution)/shard_map/all_to_all | solution.py:43
  321.6 5.2 %all-to-all-start.1 = ((bf16[14,32,2048]{2,0,1:T(8,128)(2,1)}), bf16[14,32,2048]{2,0,1:T(8,128)(2,1)}, u32[]{:S(2)}, u32[]{:S(2)}) async-start(bf16[14,32,2048]{2,0,1:T(8,128)(2,1)} %copy.38), calls=%async_computation.1 | async-start | bytes 4194304 | tf_op jit(solution)/shard_map/all_to_all | solution.py:43
  326.8 2.6 multiply_convert_fusion
  329.4 2.4 copy.46
  331.7 23.5 %all-to-all-done.1 = bf16[14,32,2048]{2,0,1:T(8,128)(2,1)} async-done(((bf16[14,32,2048]{2,0,1:T(8,128)(2,1)}), bf16[14,32,2048]{2,0,1:T(8,128)(2,1)}, u32[]{:S(2)}, u32[]{:S(2)}) %all-to-all-start.1) | async-done | bytes 1835040 | tf_op jit(solution)/shard_map/all_to_all | solution.py:43
  355.3 4.5 %all-to-all-start.3 = ((bf16[14,32,2048]{2,0,1:T(8,128)(2,1)}), bf16[14,32,2048]{2,0,1:T(8,128)(2,1)S(1)}, u32[]{:S(2)}, u32[]{:S(2)}) async-start(bf16[14,32,2048]{2,0,1:T(8,128)(2,1)} %copy.46), calls=%async_computation.3 | async-start | bytes 4194304 | tf_op jit(solution)/shard_map/all_to_all | solution.py:43
  360.9 0.8 copy.78
  362.1 0.8 copy.79
  363.2 0.8 copy.77
  364.0 24.2 %all-to-all-done.3 = bf16[14,32,2048]{2,0,1:T(8,128)(2,1)S(1)} async-done(((bf16[14,32,2048]{2,0,1:T(8,128)(2,1)}), bf16[14,32,2048]{2,0,1:T(8,128)(2,1)S(1)}, u32[]{:S(2)}, u32[]{:S(2)}) %all-to-all-start.3) | async-done | bytes 1835040 | tf_op jit(solution)/shard_map/all_to_all | solution.py:43
  388.2 3.7 convolution_divide_fusion.1
  391.9 2.2 fusion.6
  394.1 4.1 %fusion.4 = (f32[3,1,14,2048]{3,0,2,1:T(4,128)S(1)}, bf16[3,1,14,2048]{3,0,2,1:T(4,128)(2,1)S(1)}, bf16[3,1,14,2048]{3,0,2,1:T(4,128)(2,1)S(1)}, f32[3,1,14,2048]{3,0,2,1:T(4,128)S(1)}) fusion(f32[3,14,2048]{2,0,1:T(4,128)S(1)} %bitcast.69, bf16[3,14,2048]{2,0,1:T(4,128)(2,1)S(1)} %bitcast.72, f32[3,14,2048]{2,0,1:T(4,128)S(1)} %convolution_divide_fusion.1, ...), kind=kOutput, calls=%fused_computation.31 | convolution fusion | flops 6967296 | bytes 4243660 | tf_op jit(solution)/shard_map/dot_general | solution.py:80
  398.9 1.6 copy.51
  401.1 1.2 copy.50
  (60 shorter events, 5.3 us)
Async XLA Ops:
  12.5 11.5 %copy-start.9 = (bf16[24,2048]{1,0:T(8,128)(2,1)S(1)}, bf16[24,2048]{1,0:T(8,128)(2,1)}, u32[]{:S(2)}) copy-start(bf16[24,2048]{1,0:T(8,128)(2,1)} %param.6) | copy-start | bytes 294916
  12.5 88.8 %all-to-all-start = ((bf16[3,14,32,2048]{3,1,0,2:T(8,128)(2,1)}), bf16[3,14,32,2048]{3,1,0,2:T(8,128)(2,1)}, u32[]{:S(2)}, u32[]{:S(2)}) async-start(bf16[3,14,32,2048]{3,1,0,2:T(8,128)(2,1)} %bitcast.60), calls=%async_computation | async-start | bytes 12582912 | tf_op jit(solution)/shard_map/all_to_all | solution.py:20
  23.9 86.9 %all-gather.2.cloned.1.call-start = ((), (), s32[]{:S(2)}) async-start(), calls=%async_computation.4 | async-start | bytes 1671168 | tf_op jit(solution)/shard_map/all_gather | solution.py:27
  24.9 244.5 %all-reduce.2.cloned.1.call-start = ((), (), s32[]{:S(2)}) async-start(), calls=%async_computation.5 | async-start | bytes 6291456 | tf_op jit(solution)/shard_map/psum | solution.py:38
  110.8 3.3 copy-start.5
  110.8 3.3 copy-start.15
  114.1 2.0 copy-start.18
  116.1 0.7 copy-start.3
  119.6 149.9 %copy-start.2 = (bf16[384,2048]{1,0:T(8,128)(2,1)S(1)}, bf16[384,2048]{1,0:T(8,128)(2,1)}, u32[]{:S(2)}) copy-start(bf16[384,2048]{1,0:T(8,128)(2,1)} %param.7) | copy-start | bytes 4718596
  269.4 3.2 copy-start.16
  269.4 3.2 copy-start.19
  272.6 1.2 copy-start.7
  276.1 17.1 %copy-start.8 = (f32[384,448]{0,1:T(8,128)S(1)}, f32[384,448]{0,1:T(8,128)}, u32[]{:S(2)}) copy-start(f32[384,448]{0,1:T(8,128)} %copy-done.7) | copy-start | bytes 2064388
  276.1 17.1 %copy-start.17 = (bf16[384,2048]{1,0:T(8,128)(2,1)S(1)}, bf16[384,2048]{1,0:T(8,128)(2,1)}, u32[]{:S(2)}) copy-start(bf16[384,2048]{1,0:T(8,128)(2,1)} %all-gather.2.cloned.1.call-done) | copy-start | bytes 4718596
  276.2 17.1 %copy-start.20 = (f32[384,448]{0,1:T(8,128)S(1)}, f32[384,448]{0,1:T(8,128)}, u32[]{:S(2)}) copy-start(f32[384,448]{0,1:T(8,128)} %copy-done.18) | copy-start | bytes 2064388
  276.2 45.5 %all-to-all-start.2 = ((bf16[14,32,2048]{2,0,1:T(8,128)(2,1)}), bf16[14,32,2048]{2,0,1:T(8,128)(2,1)}, u32[]{:S(2)}, u32[]{:S(2)}) async-start(bf16[14,32,2048]{2,0,1:T(8,128)(2,1)} %copy.42), calls=%async_computation.2 | async-start | bytes 4194304 | tf_op jit(solution)/shard_map/all_to_all | solution.py:43
  298.0 28.7 %copy-start.1 = (f32[384,2048]{1,0:T(8,128)S(1)}, f32[384,2048]{1,0:T(8,128)}, u32[]{:S(2)}) copy-start(f32[384,2048]{1,0:T(8,128)} %all-reduce.2.cloned.1.call-done) | copy-start | bytes 9437188
  298.0 28.7 %copy-start.4 = (bf16[384,448]{0,1:T(8,128)(2,1)S(1)}, bf16[384,448]{0,1:T(8,128)(2,1)}, u32[]{:S(2)}) copy-start(bf16[384,448]{0,1:T(8,128)(2,1)} %copy-done.3) | copy-start | bytes 1032196
  321.6 33.6 %all-to-all-start.1 = ((bf16[14,32,2048]{2,0,1:T(8,128)(2,1)}), bf16[14,32,2048]{2,0,1:T(8,128)(2,1)}, u32[]{:S(2)}, u32[]{:S(2)}) async-start(bf16[14,32,2048]{2,0,1:T(8,128)(2,1)} %copy.38), calls=%async_computation.1 | async-start | bytes 4194304 | tf_op jit(solution)/shard_map/all_to_all | solution.py:43
  331.7 28.0 %copy-start.6 = (f32[3,3,14,2048]{3,2,1,0:T(8,128)S(1)}, f32[3,3,14,2048]{3,2,1,0:T(8,128)}, u32[]{:S(2)}) copy-start(f32[3,3,14,2048]{3,2,1,0:T(8,128)} %param.9) | copy-start | bytes 3096580
  355.3 32.9 %all-to-all-start.3 = ((bf16[14,32,2048]{2,0,1:T(8,128)(2,1)}), bf16[14,32,2048]{2,0,1:T(8,128)(2,1)S(1)}, u32[]{:S(2)}, u32[]{:S(2)}) async-start(bf16[14,32,2048]{2,0,1:T(8,128)(2,1)} %copy.46), calls=%async_computation.3 | async-start | bytes 4194304 | tf_op jit(solution)/shard_map/all_to_all | solution.py:43
  359.8 1.1 copy-start
  359.8 1.9 copy-start.13
  359.8 1.9 copy-start.14
  388.2 3.7 copy-start.12
  391.9 2.3 copy-start.10
  391.9 2.3 copy-start.11
Sparse Core Ops, SparseCore 0:
  27.4 64.8 all-gather.1
  119.7 149.6 all-reduce.1

commit v6 on v5

--- a/solution.py
+++ b/solution.py
@@ -4,6 +4,7 @@
 import jax.numpy as jnp
 from jax import lax
 from jax.sharding import PartitionSpec as P
+
 
 D = 2048
 FW = 7168
@@ -74,13 +75,13 @@
     new_params = []
     weighting = member.astype(jnp.bfloat16)
     for j, got in enumerate((gate_got, up_got, down_got)):
-        got, weighting_j, momentum_j, params_j = lax.optimization_barrier(
-            (got, weighting, momentum[:, j], params[:, j])
+        got, weighting_j, momentum_j, params_j, counts_j = lax.optimization_barrier(
+            (got, weighting, momentum[:, j], params[:, j], counts)
         )
         summed = lax.dot_general(
             weighting_j, got, (((0,), (1,)), ((), ())), preferred_element_type=jnp.float32
         )
-        mean_delta = summed / counts[:, None, None]
+        mean_delta = summed / counts_j[:, None, None]
         momentum_j = 0.9 * momentum_j + mean_delta
         params_j = (params_j.astype(jnp.float32) - 0.7 * (mean_delta + 0.9 * momentum_j)).astype(
             jnp.bfloat16

time: 410 us -> 410 us (level)
  no operation moved by 1% of the time
where the time goes in v6:
time: 410 us; the launch traced here: 409 us
  waiting for transfers between devices  298 us (73%)
  starting transfers between devices  38.2 us (9%)
  local copies, waits for them, and re-layouts  28.8 us (7%)
  matrix products  27.3 us (7%)
  between operations  14.4 us (4%)
    psum x1, waiting for transfers between devices, per_device(): output = lax.psum(partial_out, 'tensor')  150 us
    all_to_all x1, waiting for transfers between devices, per_device(): lax.all_to_all(picked, 'path', split_axis=2, concat_axis=2, tiled=True)  76.3 us
    all_to_all x3, waiting for transfers between devices, send_back(): lax.all_to_all(delta.reshape(piece_shape), 'path', split_axis=1, concat_a...  71.4 us
    all_to_all x3, starting transfers between devices, send_back(): lax.all_to_all(delta.reshape(piece_shape), 'path', split_axis=1, concat_a...  26.7 us
    all_to_all x1, starting transfers between devices, per_device(): lax.all_to_all(picked, 'path', split_axis=2, concat_axis=2, tiled=True)  11.5 us
    dot_general x3, matrix products, per_device(): lax.dot_general(weighting_j, got, (((0,), (1,)), ((), ())), preferred_ele...  10.1 us
    slice x4, local copies, waits for them, and re-layouts, per_device(): gate_rows, up_rows, down_rows = (rows[0], rows[1], rows[2])  9.49 us
  transfers between devices with their start and end apart: 6, of which 5 were waited for; matrix products, arithmetic and copies ran while one was open for 6% of the time, Pallas kernels for 0%

profile of v6, /device:TPU:1, one launch (start us, length us, event | category | flops | bytes accessed | tf_op | source)
XLA Modules:
  0.0 409.1 jit_solution(4344214532562497575)
XLA Ops:
  7.8 4.6 %gather_fusion = bf16[32,3,14,2048]{3,2,1,0:T(8,128)(2,1)} fusion(bf16[3,3,14,2048]{3,2,1,0:T(8,128)(2,1)} %param.8, s32[1024]{0:T(1024)S(1)} %pad_clamp_fusion), kind=kCustom, calls=%fused_computation | custom fusion | bytes 11010176 | tf_op jit(solution)/shard_map/jit(_take)/gather | solution.py:20
  12.5 11.5 %all-to-all-start = ((bf16[3,14,32,2048]{3,1,0,2:T(8,128)(2,1)}), bf16[3,14,32,2048]{3,1,0,2:T(8,128)(2,1)}, u32[]{:S(2)}, u32[]{:S(2)}) async-start(bf16[3,14,32,2048]{3,1,0,2:T(8,128)(2,1)} %bitcast.60), calls=%async_computation | async-start | bytes 12582912 | tf_op jit(solution)/shard_map/all_to_all | solution.py:21
  24.9 76.3 %all-to-all-done = bf16[3,14,32,2048]{3,1,0,2:T(8,128)(2,1)} async-done(((bf16[3,14,32,2048]{3,1,0,2:T(8,128)(2,1)}), bf16[3,14,32,2048]{3,1,0,2:T(8,128)(2,1)}, u32[]{:S(2)}, u32[]{:S(2)}) %all-to-all-start) | async-done | bytes 5505056 | tf_op jit(solution)/shard_map/all_to_all | solution.py:21
  101.3 4.0 fusion.19
  105.3 2.2 copy.35
  107.5 2.3 copy.36
  109.8 1.0 copy.37
  110.8 3.3 convolution_multiply_fusion.3
  114.1 2.0 multiply_convert_fusion.6
  116.8 2.7 convolution_multiply_fusion
  119.6 149.8 %all-reduce.2.cloned.1.call-done = f32[384,2048]{1,0:T(8,128)} async-done(((f32[384,2048]{1,0:T(8,128)}), f32[384,2048]{1,0:T(8,128)}) %all-reduce.2.cloned.1.call-update) | async-done | bytes 3145744 | tf_op jit(solution)/shard_map/psum | solution.py:39
  269.4 3.2 convolution_multiply_fusion.1
  272.6 1.1 multiply_convert_fusion.1
  273.8 2.3 copy.42
  276.2 17.1 %all-to-all-start.2 = ((bf16[14,32,2048]{2,0,1:T(8,128)(2,1)}), bf16[14,32,2048]{2,0,1:T(8,128)(2,1)}, u32[]{:S(2)}, u32[]{:S(2)}) async-start(bf16[14,32,2048]{2,0,1:T(8,128)(2,1)} %copy.42), calls=%async_computation.2 | async-start | bytes 4194304 | tf_op jit(solution)/shard_map/all_to_all | solution.py:44
  293.3 2.4 multiply_convert_fusion.2
  295.6 2.4 copy.38
  298.1 23.6 %all-to-all-done.2 = bf16[14,32,2048]{2,0,1:T(8,128)(2,1)} async-done(((bf16[14,32,2048]{2,0,1:T(8,128)(2,1)}), bf16[14,32,2048]{2,0,1:T(8,128)(2,1)}, u32[]{:S(2)}, u32[]{:S(2)}) %all-to-all-start.2) | async-done | bytes 1835040 | tf_op jit(solution)/shard_map/all_to_all | solution.py:44
  321.6 5.2 %all-to-all-start.1 = ((bf16[14,32,2048]{2,0,1:T(8,128)(2,1)}), bf16[14,32,2048]{2,0,1:T(8,128)(2,1)}, u32[]{:S(2)}, u32[]{:S(2)}) async-start(bf16[14,32,2048]{2,0,1:T(8,128)(2,1)} %copy.38), calls=%async_computation.1 | async-start | bytes 4194304 | tf_op jit(solution)/shard_map/all_to_all | solution.py:44
  326.8 2.6 multiply_convert_fusion
  329.4 2.4 copy.46
  331.7 23.5 %all-to-all-done.1 = bf16[14,32,2048]{2,0,1:T(8,128)(2,1)} async-done(((bf16[14,32,2048]{2,0,1:T(8,128)(2,1)}), bf16[14,32,2048]{2,0,1:T(8,128)(2,1)}, u32[]{:S(2)}, u32[]{:S(2)}) %all-to-all-start.1) | async-done | bytes 1835040 | tf_op jit(solution)/shard_map/all_to_all | solution.py:44
  355.3 4.5 %all-to-all-start.3 = ((bf16[14,32,2048]{2,0,1:T(8,128)(2,1)}), bf16[14,32,2048]{2,0,1:T(8,128)(2,1)S(1)}, u32[]{:S(2)}, u32[]{:S(2)}) async-start(bf16[14,32,2048]{2,0,1:T(8,128)(2,1)} %copy.46), calls=%async_computation.3 | async-start | bytes 4194304 | tf_op jit(solution)/shard_map/all_to_all | solution.py:44
  360.9 0.8 copy.78
  362.0 0.8 copy.79
  363.0 0.8 copy.77
  363.9 24.3 %all-to-all-done.3 = bf16[14,32,2048]{2,0,1:T(8,128)(2,1)S(1)} async-done(((bf16[14,32,2048]{2,0,1:T(8,128)(2,1)}), bf16[14,32,2048]{2,0,1:T(8,128)(2,1)S(1)}, u32[]{:S(2)}, u32[]{:S(2)}) %all-to-all-start.3) | async-done | bytes 1835040 | tf_op jit(solution)/shard_map/all_to_all | solution.py:44
  388.2 3.7 convolution_divide_fusion.1
  391.9 2.2 fusion.6
  394.1 4.1 %fusion.4 = (f32[3,1,14,2048]{3,0,2,1:T(4,128)S(1)}, bf16[3,1,14,2048]{3,0,2,1:T(4,128)(2,1)S(1)}, bf16[3,1,14,2048]{3,0,2,1:T(4,128)(2,1)S(1)}, f32[3,1,14,2048]{3,0,2,1:T(4,128)S(1)}) fusion(f32[3,14,2048]{2,0,1:T(4,128)S(1)} %bitcast.69, bf16[3,14,2048]{2,0,1:T(4,128)(2,1)S(1)} %bitcast.72, f32[3,14,2048]{2,0,1:T(4,128)S(1)} %convolution_divide_fusion.1, ...), kind=kOutput, calls=%fused_computation.31 | convolution fusion | flops 6967296 | bytes 4243660 | tf_op jit(solution)/shard_map/dot_general | solution.py:81
  398.9 1.6 copy.51
  401.1 1.2 copy.50
  (60 shorter events, 5.2 us)
Async XLA Ops:
  12.5 11.5 %copy-start.9 = (bf16[24,2048]{1,0:T(8,128)(2,1)S(1)}, bf16[24,2048]{1,0:T(8,128)(2,1)}, u32[]{:S(2)}) copy-start(bf16[24,2048]{1,0:T(8,128)(2,1)} %param.6) | copy-start | bytes 294916
  12.5 88.8 %all-to-all-start = ((bf16[3,14,32,2048]{3,1,0,2:T(8,128)(2,1)}), bf16[3,14,32,2048]{3,1,0,2:T(8,128)(2,1)}, u32[]{:S(2)}, u32[]{:S(2)}) async-start(bf16[3,14,32,2048]{3,1,0,2:T(8,128)(2,1)} %bitcast.60), calls=%async_computation | async-start | bytes 12582912 | tf_op jit(solution)/shard_map/all_to_all | solution.py:21
  23.9 86.9 %all-gather.2.cloned.1.call-start = ((), (), s32[]{:S(2)}) async-start(), calls=%async_computation.4 | async-start | bytes 1671168 | tf_op jit(solution)/shard_map/all_gather | solution.py:28
  24.9 244.5 %all-reduce.2.cloned.1.call-start = ((), (), s32[]{:S(2)}) async-start(), calls=%async_computation.5 | async-start | bytes 6291456 | tf_op jit(solution)/shard_map/psum | solution.py:39
  110.8 3.3 copy-start.5
  110.8 3.3 copy-start.15
  114.1 2.0 copy-start.18
  116.1 0.7 copy-start.3
  119.6 149.9 %copy-start.2 = (bf16[384,2048]{1,0:T(8,128)(2,1)S(1)}, bf16[384,2048]{1,0:T(8,128)(2,1)}, u32[]{:S(2)}) copy-start(bf16[384,2048]{1,0:T(8,128)(2,1)} %param.7) | copy-start | bytes 4718596
  269.4 3.2 copy-start.16
  269.4 3.2 copy-start.19
  272.6 1.2 copy-start.7
  276.1 17.1 %copy-start.8 = (f32[384,448]{0,1:T(8,128)S(1)}, f32[384,448]{0,1:T(8,128)}, u32[]{:S(2)}) copy-start(f32[384,448]{0,1:T(8,128)} %copy-done.7) | copy-start | bytes 2064388
  276.1 17.1 %copy-start.17 = (bf16[384,2048]{1,0:T(8,128)(2,1)S(1)}, bf16[384,2048]{1,0:T(8,128)(2,1)}, u32[]{:S(2)}) copy-start(bf16[384,2048]{1,0:T(8,128)(2,1)} %all-gather.2.cloned.1.call-done) | copy-start | bytes 4718596
  276.2 17.1 %copy-start.20 = (f32[384,448]{0,1:T(8,128)S(1)}, f32[384,448]{0,1:T(8,128)}, u32[]{:S(2)}) copy-start(f32[384,448]{0,1:T(8,128)} %copy-done.18) | copy-start | bytes 2064388
  276.2 45.5 %all-to-all-start.2 = ((bf16[14,32,2048]{2,0,1:T(8,128)(2,1)}), bf16[14,32,2048]{2,0,1:T(8,128)(2,1)}, u32[]{:S(2)}, u32[]{:S(2)}) async-start(bf16[14,32,2048]{2,0,1:T(8,128)(2,1)} %copy.42), calls=%async_computation.2 | async-start | bytes 4194304 | tf_op jit(solution)/shard_map/all_to_all | solution.py:44
  298.0 28.7 %copy-start.1 = (f32[384,2048]{1,0:T(8,128)S(1)}, f32[384,2048]{1,0:T(8,128)}, u32[]{:S(2)}) copy-start(f32[384,2048]{1,0:T(8,128)} %all-reduce.2.cloned.1.call-done) | copy-start | bytes 9437188
  298.0 28.7 %copy-start.4 = (bf16[384,448]{0,1:T(8,128)(2,1)S(1)}, bf16[384,448]{0,1:T(8,128)(2,1)}, u32[]{:S(2)}) copy-start(bf16[384,448]{0,1:T(8,128)(2,1)} %copy-done.3) | copy-start | bytes 1032196
  321.6 33.6 %all-to-all-start.1 = ((bf16[14,32,2048]{2,0,1:T(8,128)(2,1)}), bf16[14,32,2048]{2,0,1:T(8,128)(2,1)}, u32[]{:S(2)}, u32[]{:S(2)}) async-start(bf16[14,32,2048]{2,0,1:T(8,128)(2,1)} %copy.38), calls=%async_computation.1 | async-start | bytes 4194304 | tf_op jit(solution)/shard_map/all_to_all | solution.py:44
  331.7 28.0 %copy-start.13 = (s32[32]{0:T(128)S(1)}, s32[32]{0:T(128)}, u32[]{:S(2)}) copy-start(s32[32]{0:T(128)} %param.11) | copy-start | bytes 388
  331.7 28.0 %copy-start.14 = (s32[32]{0:T(128)S(1)}, s32[32]{0:T(128)}, u32[]{:S(2)}) copy-start(s32[32]{0:T(128)} %param.10) | copy-start | bytes 388
  331.7 28.2 %copy-start.6 = (f32[3,3,14,2048]{3,2,1,0:T(8,128)S(1)}, f32[3,3,14,2048]{3,2,1,0:T(8,128)}, u32[]{:S(2)}) copy-start(f32[3,3,14,2048]{3,2,1,0:T(8,128)} %param.9) | copy-start | bytes 3096580
  355.3 32.9 %all-to-all-start.3 = ((bf16[14,32,2048]{2,0,1:T(8,128)(2,1)}), bf16[14,32,2048]{2,0,1:T(8,128)(2,1)S(1)}, u32[]{:S(2)}, u32[]{:S(2)}) async-start(bf16[14,32,2048]{2,0,1:T(8,128)(2,1)} %copy.46), calls=%async_computation.3 | async-start | bytes 4194304 | tf_op jit(solution)/shard_map/all_to_all | solution.py:44
  359.8 1.1 copy-start
  388.2 3.7 copy-start.12
  391.9 2.3 copy-start.10
  391.9 2.3 copy-start.11
Sparse Core Ops, SparseCore 0:
  27.4 64.8 all-gather.1
  119.7 149.6 all-reduce.1

commit v7 on v6

--- a/solution.py
+++ b/solution.py
@@ -66,7 +66,14 @@
         lax.dot_general(up_grad, normed, contract_first, preferred_element_type=jnp.float32)
         / math.sqrt(D)
     ).astype(jnp.bfloat16)
-    up_got = send_back(up_delta)
+    split = block_rows - block_rows // 3
+    up_pieces = up_delta.reshape(piece_shape)
+
+    def send_rows(piece):
+        return lax.all_to_all(piece, "path", split_axis=1, concat_axis=1, tiled=True)
+
+    up_got_a = send_rows(up_pieces[:split])
+    up_got_b = send_rows(up_pieces[split:])
     member = (path_module[:, None] == jnp.arange(module_count, dtype=jnp.int32)[None, :]).astype(
         jnp.int32
     ) * path_alive[:, None]
@@ -74,9 +81,15 @@
     new_momentum = []
     new_params = []
     weighting = member.astype(jnp.bfloat16)
-    for j, got in enumerate((gate_got, up_got, down_got)):
+    parts = (
+        (gate_got, 0, slice(None)),
+        (up_got_a, 1, slice(0, split)),
+        (up_got_b, 1, slice(split, None)),
+        (down_got, 2, slice(None)),
+    )
+    for got, j, rows in parts:
         got, weighting_j, momentum_j, params_j, counts_j = lax.optimization_barrier(
-            (got, weighting, momentum[:, j], params[:, j], counts)
+            (got, weighting, momentum[:, j, rows], params[:, j, rows], counts)
         )
         summed = lax.dot_general(
             weighting_j, got, (((0,), (1,)), ((), ())), preferred_element_type=jnp.float32
@@ -88,6 +101,8 @@
         )
         new_momentum.append(momentum_j)
         new_params.append(params_j)
+    new_momentum = [new_momentum[0], jnp.concatenate(new_momentum[1:3], axis=1), new_momentum[3]]
+    new_params = [new_params[0], jnp.concatenate(new_params[1:3], axis=1), new_params[3]]
     new_momentum = jnp.stack(new_momentum, axis=1)
     new_params = jnp.stack(new_params, axis=1)
     return (new_params, new_momentum)

time: 410 us -> 420 us (1.024)
  starting transfers between devices: 38.2 us -> 42.7 us
  local copies, waits for them, and re-layouts: 28.8 us -> 33.3 us
    all_to_all x0 -> x2, waiting for transfers between devices: none -> 32.4 us  [send_rows(): lax.all_to_all(piece, 'path', split_axis=1, concat_axis=1, tiled=True)]
    all_to_all x3 -> x2, waiting for transfers between devices: 71.4 us -> 39.1 us  [send_back(): lax.all_to_all(delta.reshape(piece_shape), 'path', split_axis=1, concat_a...]
    all_to_all x0 -> x2, starting transfers between devices: none -> 21.5 us  [send_rows(): lax.all_to_all(piece, 'path', split_axis=1, concat_axis=1, tiled=True)]
    all_to_all x3 -> x2, starting transfers between devices: 26.7 us -> 9.64 us  [send_back(): lax.all_to_all(delta.reshape(piece_shape), 'path', split_axis=1, concat_a...]
    slice x2 -> x10, local copies, waits for them, and re-layouts: 0.12 us -> 6.81 us  [the longest x3 3.31 us: per_device(): momentum[:, j, rows]]
    dot_general x3 -> x4, matrix products: 10.1 us -> 11.1 us  [per_device(): lax.dot_general(weighting_j, got, (((0,), (1,)), ((), ())), preferred_ele...]
  transfers between devices with their start and end apart: 6 -> 7, of which waited for: 5 -> 6; matrix products, arithmetic and copies ran while one was open for 6% -> 8% of each run, Pallas kernels for 0% -> 0%
where the time goes in v7:
time: 420 us
  waiting for transfers between devices  298 us (71%)
  starting transfers between devices  42.7 us (10%)
  local copies, waits for them, and re-layouts  33.3 us (8%)
  matrix products  28.5 us (7%)
  between operations  14.4 us (3%)
    psum x1, waiting for transfers between devices, per_device(): output = lax.psum(partial_out, 'tensor')  150 us
    all_to_all x1, waiting for transfers between devices, per_device(): lax.all_to_all(picked, 'path', split_axis=2, concat_axis=2, tiled=True)  76.3 us
    all_to_all x2, waiting for transfers between devices, send_back(): lax.all_to_all(delta.reshape(piece_shape), 'path', split_axis=1, concat_a...  39.1 us
    all_to_all x2, waiting for transfers between devices, send_rows(): lax.all_to_all(piece, 'path', split_axis=1, concat_axis=1, tiled=True)  32.4 us
    all_to_all x2, starting transfers between devices, send_rows(): lax.all_to_all(piece, 'path', split_axis=1, concat_axis=1, tiled=True)  21.5 us
    all_to_all x1, starting transfers between devices, per_device(): lax.all_to_all(picked, 'path', split_axis=2, concat_axis=2, tiled=True)  11.5 us
    dot_general x4, matrix products, per_device(): lax.dot_general(weighting_j, got, (((0,), (1,)), ((), ())), preferred_ele...  11.1 us
    all_to_all x2, starting transfers between devices, send_back(): lax.all_to_all(delta.reshape(piece_shape), 'path', split_axis=1, concat_a...  9.64 us
  transfers between devices with their start and end apart: 7, of which 6 were waited for; matrix products, arithmetic and copies ran while one was open for 8% of the time, Pallas kernels for 0%

profile of v7, /device:TPU:1, one launch (start us, length us, event | category | flops | bytes accessed | tf_op | source)
XLA Modules:
  0.0 419.6 jit_solution(8838311776757902504)
XLA Ops:
  7.8 4.6 %gather_fusion = bf16[32,3,14,2048]{3,2,1,0:T(8,128)(2,1)} fusion(bf16[3,3,14,2048]{3,2,1,0:T(8,128)(2,1)} %param.8, s32[1024]{0:T(1024)S(1)} %pad_clamp_fusion), kind=kCustom, calls=%fused_computation | custom fusion | bytes 11010176 | tf_op jit(solution)/shard_map/jit(_take)/gather | solution.py:20
  12.5 11.5 %all-to-all-start = ((bf16[3,14,32,2048]{3,1,0,2:T(8,128)(2,1)}), bf16[3,14,32,2048]{3,1,0,2:T(8,128)(2,1)}, u32[]{:S(2)}, u32[]{:S(2)}) async-start(bf16[3,14,32,2048]{3,1,0,2:T(8,128)(2,1)} %bitcast.72), calls=%async_computation | async-start | bytes 12582912 | tf_op jit(solution)/shard_map/all_to_all | solution.py:21
  24.9 76.3 %all-to-all-done = bf16[3,14,32,2048]{3,1,0,2:T(8,128)(2,1)} async-done(((bf16[3,14,32,2048]{3,1,0,2:T(8,128)(2,1)}), bf16[3,14,32,2048]{3,1,0,2:T(8,128)(2,1)}, u32[]{:S(2)}, u32[]{:S(2)}) %all-to-all-start) | async-done | bytes 5505056 | tf_op jit(solution)/shard_map/all_to_all | solution.py:21
  101.3 4.0 fusion.19
  105.3 2.2 copy.41
  107.5 2.3 copy.42
  110.8 3.3 convolution_multiply_fusion.3
  114.1 2.0 multiply_convert_fusion.6
  116.9 2.7 convolution_multiply_fusion
  119.6 149.8 %all-reduce.2.cloned.1.call-done = f32[384,2048]{1,0:T(8,128)} async-done(((f32[384,2048]{1,0:T(8,128)}), f32[384,2048]{1,0:T(8,128)}) %all-reduce.2.cloned.1.call-update) | async-done | bytes 3145744 | tf_op jit(solution)/shard_map/psum | solution.py:39
  269.4 3.2 convolution_multiply_fusion.1
  273.9 1.2 copy.52
  275.1 16.8 %all-to-all-start.3 = ((bf16[4,32,2048]{2,0,1:T(4,128)(2,1)}), bf16[4,32,2048]{2,0,1:T(4,128)(2,1)}, u32[]{:S(2)}, u32[]{:S(2)}) async-start(bf16[4,32,2048]{2,0,1:T(4,128)(2,1)} %copy.52), calls=%async_computation.3 | async-start | bytes 1048576 | tf_op jit(solution)/shard_map/all_to_all | solution.py:73
  292.0 2.1 copy.48
  294.1 9.4 %all-to-all-done.3 = bf16[4,32,2048]{2,0,1:T(4,128)(2,1)} async-done(((bf16[4,32,2048]{2,0,1:T(4,128)(2,1)}), bf16[4,32,2048]{2,0,1:T(4,128)(2,1)}, u32[]{:S(2)}, u32[]{:S(2)}) %all-to-all-start.3) | async-done | bytes 524320 | tf_op jit(solution)/shard_map/all_to_all | solution.py:73
  303.5 4.7 %all-to-all-start.2 = ((bf16[10,32,2048]{2,0,1:T(8,128)(2,1)}), bf16[10,32,2048]{2,0,1:T(8,128)(2,1)}, u32[]{:S(2)}, u32[]{:S(2)}) async-start(bf16[10,32,2048]{2,0,1:T(8,128)(2,1)} %copy.48), calls=%async_computation.2 | async-start | bytes 4194304 | tf_op jit(solution)/shard_map/all_to_all | solution.py:73
  308.3 2.6 multiply_convert_fusion
  310.8 2.4 copy.56
  313.2 23.0 %all-to-all-done.2 = bf16[10,32,2048]{2,0,1:T(8,128)(2,1)} async-done(((bf16[10,32,2048]{2,0,1:T(8,128)(2,1)}), bf16[10,32,2048]{2,0,1:T(8,128)(2,1)}, u32[]{:S(2)}, u32[]{:S(2)}) %all-to-all-start.2) | async-done | bytes 1310752 | tf_op jit(solution)/shard_map/all_to_all | solution.py:73
  336.2 4.5 %all-to-all-start.4 = ((bf16[14,32,2048]{2,0,1:T(8,128)(2,1)}), bf16[14,32,2048]{2,0,1:T(8,128)(2,1)S(1)}, u32[]{:S(2)}, u32[]{:S(2)}) async-start(bf16[14,32,2048]{2,0,1:T(8,128)(2,1)} %copy.56), calls=%async_computation.4 | async-start | bytes 4194304 | tf_op jit(solution)/shard_map/all_to_all | solution.py:44
  340.8 1.2 slice.55
  344.2 2.6 multiply_convert_fusion.2
  346.8 2.3 copy.44
  349.2 20.0 %all-to-all-done.4 = bf16[14,32,2048]{2,0,1:T(8,128)(2,1)S(1)} async-done(((bf16[14,32,2048]{2,0,1:T(8,128)(2,1)}), bf16[14,32,2048]{2,0,1:T(8,128)(2,1)S(1)}, u32[]{:S(2)}, u32[]{:S(2)}) %all-to-all-start.4) | async-done | bytes 1835040 | tf_op jit(solution)/shard_map/all_to_all | solution.py:44
  369.1 5.2 %all-to-all-start.1 = ((bf16[14,32,2048]{2,0,1:T(8,128)(2,1)}), bf16[14,32,2048]{2,0,1:T(8,128)(2,1)}, u32[]{:S(2)}, u32[]{:S(2)}) async-start(bf16[14,32,2048]{2,0,1:T(8,128)(2,1)} %copy.44), calls=%async_computation.1 | async-start | bytes 4194304 | tf_op jit(solution)/shard_map/all_to_all | solution.py:44
  378.5 1.7 multiply_add_fusion.3
  380.2 3.2 multiply_add_fusion.2
  383.6 19.1 %all-to-all-done.1 = bf16[14,32,2048]{2,0,1:T(8,128)(2,1)} async-done(((bf16[14,32,2048]{2,0,1:T(8,128)(2,1)}), bf16[14,32,2048]{2,0,1:T(8,128)(2,1)}, u32[]{:S(2)}, u32[]{:S(2)}) %all-to-all-start.1) | async-done | bytes 1835040 | tf_op jit(solution)/shard_map/all_to_all | solution.py:44
  402.8 2.1 convolution_divide_fusion
  404.9 4.1 fusion.5
  409.4 1.6 copy.61
  411.6 1.2 copy.60
  (72 shorter events, 12.3 us)
Async XLA Ops:
  12.5 11.5 %copy-start.9 = (bf16[24,2048]{1,0:T(8,128)(2,1)S(1)}, bf16[24,2048]{1,0:T(8,128)(2,1)}, u32[]{:S(2)}) copy-start(bf16[24,2048]{1,0:T(8,128)(2,1)} %param.6) | copy-start | bytes 294916
  12.5 88.8 %all-to-all-start = ((bf16[3,14,32,2048]{3,1,0,2:T(8,128)(2,1)}), bf16[3,14,32,2048]{3,1,0,2:T(8,128)(2,1)}, u32[]{:S(2)}, u32[]{:S(2)}) async-start(bf16[3,14,32,2048]{3,1,0,2:T(8,128)(2,1)} %bitcast.72), calls=%async_computation | async-start | bytes 12582912 | tf_op jit(solution)/shard_map/all_to_all | solution.py:21
  23.9 86.9 %all-gather.2.cloned.1.call-start = ((), (), s32[]{:S(2)}) async-start(), calls=%async_computation.5 | async-start | bytes 1671168 | tf_op jit(solution)/shard_map/all_gather | solution.py:28
  24.9 244.5 %all-reduce.2.cloned.1.call-start = ((), (), s32[]{:S(2)}) async-start(), calls=%async_computation.6 | async-start | bytes 6291456 | tf_op jit(solution)/shard_map/psum | solution.py:39
  110.8 3.3 copy-start.5
  110.8 3.3 copy-start.15
  114.1 2.0 copy-start.18
  116.1 0.7 copy-start.3
  119.6 149.9 %copy-start.2 = (bf16[384,2048]{1,0:T(8,128)(2,1)S(1)}, bf16[384,2048]{1,0:T(8,128)(2,1)}, u32[]{:S(2)}) copy-start(bf16[384,2048]{1,0:T(8,128)(2,1)} %param.7) | copy-start | bytes 4718596
  269.4 3.2 copy-start.16
  269.4 3.2 copy-start.19
  272.7 1.2 copy-start.6
  275.1 28.4 %all-to-all-start.3 = ((bf16[4,32,2048]{2,0,1:T(4,128)(2,1)}), bf16[4,32,2048]{2,0,1:T(4,128)(2,1)}, u32[]{:S(2)}, u32[]{:S(2)}) async-start(bf16[4,32,2048]{2,0,1:T(4,128)(2,1)} %copy.52), calls=%async_computation.3 | async-start | bytes 1048576 | tf_op jit(solution)/shard_map/all_to_all | solution.py:73
  294.1 14.2 %copy-start.1 = (f32[384,2048]{1,0:T(8,128)S(1)}, f32[384,2048]{1,0:T(8,128)}, u32[]{:S(2)}) copy-start(f32[384,2048]{1,0:T(8,128)} %all-reduce.2.cloned.1.call-done) | copy-start | bytes 9437188
  294.1 14.2 %copy-start.4 = (bf16[384,448]{0,1:T(8,128)(2,1)S(1)}, bf16[384,448]{0,1:T(8,128)(2,1)}, u32[]{:S(2)}) copy-start(bf16[384,448]{0,1:T(8,128)(2,1)} %copy-done.3) | copy-start | bytes 1032196
  303.5 32.7 %all-to-all-start.2 = ((bf16[10,32,2048]{2,0,1:T(8,128)(2,1)}), bf16[10,32,2048]{2,0,1:T(8,128)(2,1)}, u32[]{:S(2)}, u32[]{:S(2)}) async-start(bf16[10,32,2048]{2,0,1:T(8,128)(2,1)} %copy.48), calls=%async_computation.2 | async-start | bytes 4194304 | tf_op jit(solution)/shard_map/all_to_all | solution.py:73
  313.2 27.5 %copy-start = (bf16[3,3,14,2048]{3,2,1,0:T(8,128)(2,1)S(1)}, bf16[3,3,14,2048]{3,2,1,0:T(8,128)(2,1)}, u32[]{:S(2)}) copy-start(bf16[3,3,14,2048]{3,2,1,0:T(8,128)(2,1)} %param.8) | copy-start | bytes 1548292
  313.2 29.7 %copy-start.13 = (s32[32]{0:T(128)S(1)}, s32[32]{0:T(128)}, u32[]{:S(2)}) copy-start(s32[32]{0:T(128)} %param.11) | copy-start | bytes 388
  313.2 29.7 %copy-start.14 = (s32[32]{0:T(128)S(1)}, s32[32]{0:T(128)}, u32[]{:S(2)}) copy-start(s32[32]{0:T(128)} %param.10) | copy-start | bytes 388
  336.2 32.9 %all-to-all-start.4 = ((bf16[14,32,2048]{2,0,1:T(8,128)(2,1)}), bf16[14,32,2048]{2,0,1:T(8,128)(2,1)S(1)}, u32[]{:S(2)}, u32[]{:S(2)}) async-start(bf16[14,32,2048]{2,0,1:T(8,128)(2,1)} %copy.56), calls=%async_computation.4 | async-start | bytes 4194304 | tf_op jit(solution)/shard_map/all_to_all | solution.py:44
  340.7 3.5 copy-start.7
  340.7 3.5 copy-start.17
  369.1 33.6 %all-to-all-start.1 = ((bf16[14,32,2048]{2,0,1:T(8,128)(2,1)}), bf16[14,32,2048]{2,0,1:T(8,128)(2,1)}, u32[]{:S(2)}, u32[]{:S(2)}) async-start(bf16[14,32,2048]{2,0,1:T(8,128)(2,1)} %copy.44), calls=%async_computation.1 | async-start | bytes 4194304 | tf_op jit(solution)/shard_map/all_to_all | solution.py:44
  375.8 4.4 %copy-start.10 = (f32[3,1,10,2048]{3,0,2,1:T(4,128)S(1)}, f32[3,1,10,2048]{3,0,2,1:T(4,128)}, u32[]{:S(2)}) copy-start(f32[3,1,10,2048]{3,0,2,1:T(4,128)} %copy.94) | copy-start | bytes 737284
  402.8 2.1 copy-start.8
  402.8 2.1 copy-start.11
  402.8 2.1 copy-start.12
Sparse Core Ops, SparseCore 0:
  27.4 64.8 all-gather.1
  119.7 149.6 all-reduce.1

commit v8 on v6

--- a/solution.py
+++ b/solution.py
@@ -71,10 +71,10 @@
         jnp.int32
     ) * path_alive[:, None]
     counts = jnp.sum(member, axis=0).astype(jnp.float32)
-    new_momentum = []
-    new_params = []
+    new_momentum = momentum
+    new_params = params
     weighting = member.astype(jnp.bfloat16)
-    for j, got in enumerate((gate_got, up_got, down_got)):
+    for j, got in ((0, gate_got), (2, down_got), (1, up_got)):
         got, weighting_j, momentum_j, params_j, counts_j = lax.optimization_barrier(
             (got, weighting, momentum[:, j], params[:, j], counts)
         )
@@ -86,10 +86,8 @@
         params_j = (params_j.astype(jnp.float32) - 0.7 * (mean_delta + 0.9 * momentum_j)).astype(
             jnp.bfloat16
         )
-        new_momentum.append(momentum_j)
-        new_params.append(params_j)
-    new_momentum = jnp.stack(new_momentum, axis=1)
-    new_params = jnp.stack(new_params, axis=1)
+        new_momentum = new_momentum.at[:, j].set(momentum_j)
+        new_params = new_params.at[:, j].set(params_j)
     return (new_params, new_momentum)
 
 

time: 410 us -> 408 us (level)
  transfers between devices with their start and end apart: 6 -> 6, of which waited for: 5 -> 5; matrix products, arithmetic and copies ran while one was open for 6% -> 7% of each run, Pallas kernels for 0% -> 0%
where the time goes in v8:
time: 408 us; the launch traced here: 407 us
  waiting for transfers between devices  295 us (72%)
  starting transfers between devices  38.1 us (9%)
  matrix products  30.2 us (7%)
  local copies, waits for them, and re-layouts  28.6 us (7%)
  between operations  14.4 us (4%)
    psum x1, waiting for transfers between devices, per_device(): output = lax.psum(partial_out, 'tensor')  150 us
    all_to_all x1, waiting for transfers between devices, per_device(): lax.all_to_all(picked, 'path', split_axis=2, concat_axis=2, tiled=True)  76.3 us
    all_to_all x3, waiting for transfers between devices, send_back(): lax.all_to_all(delta.reshape(piece_shape), 'path', split_axis=1, concat_a...  68.4 us
    all_to_all x3, starting transfers between devices, send_back(): lax.all_to_all(delta.reshape(piece_shape), 'path', split_axis=1, concat_a...  26.6 us
    dot_general x3, matrix products, per_device(): lax.dot_general(weighting_j, got, (((0,), (1,)), ((), ())), preferred_ele...  11.5 us
    all_to_all x1, starting transfers between devices, per_device(): lax.all_to_all(picked, 'path', split_axis=2, concat_axis=2, tiled=True)  11.5 us
    slice x4, local copies, waits for them, and re-layouts, per_device(): gate_rows, up_rows, down_rows = (rows[0], rows[1], rows[2])  9.49 us
  transfers between devices with their start and end apart: 6, of which 5 were waited for; matrix products, arithmetic and copies ran while one was open for 7% of the time, Pallas kernels for 0%

profile of v8, /device:TPU:1, one launch (start us, length us, event | category | flops | bytes accessed | tf_op | source)
XLA Modules:
  0.0 406.9 jit_solution(12654283415557406077)
XLA Ops:
  7.2 1.2 copy.113
  8.6 1.0 copy.114
  9.6 3.6 gather_fusion
  13.2 11.5 %all-to-all-start = ((bf16[3,14,32,2048]{3,1,0,2:T(8,128)(2,1)}), bf16[3,14,32,2048]{3,1,0,2:T(8,128)(2,1)}, u32[]{:S(2)}, u32[]{:S(2)}) async-start(bf16[3,14,32,2048]{3,1,0,2:T(8,128)(2,1)} %bitcast.62), calls=%async_computation | async-start | bytes 12582912 | tf_op jit(solution)/shard_map/all_to_all | solution.py:21
  24.9 0.7 fusion.12
  25.7 76.3 %all-to-all-done = bf16[3,14,32,2048]{3,1,0,2:T(8,128)(2,1)} async-done(((bf16[3,14,32,2048]{3,1,0,2:T(8,128)(2,1)}), bf16[3,14,32,2048]{3,1,0,2:T(8,128)(2,1)}, u32[]{:S(2)}, u32[]{:S(2)}) %all-to-all-start) | async-done | bytes 5505056 | tf_op jit(solution)/shard_map/all_to_all | solution.py:21
  102.0 4.0 fusion.19
  106.0 2.2 copy.47
  108.2 2.3 copy.48
  110.5 1.0 copy.49
  111.6 3.3 convolution_multiply_fusion.3
  114.9 2.0 multiply_convert_fusion.6
  116.9 2.7 convolution_multiply_fusion
  119.6 149.8 %all-reduce.2.cloned.1.call-done = f32[384,2048]{1,0:T(8,128)} async-done(((f32[384,2048]{1,0:T(8,128)}), f32[384,2048]{1,0:T(8,128)}) %all-reduce.2.cloned.1.call-update) | async-done | bytes 3145744 | tf_op jit(solution)/shard_map/psum | solution.py:39
  269.4 3.6 convolution_multiply_fusion.1
  273.1 1.3 multiply_convert_fusion.2
  274.4 2.3 copy.50
  276.7 16.9 %all-to-all-start.1 = ((bf16[14,32,2048]{2,0,1:T(8,128)(2,1)}), bf16[14,32,2048]{2,0,1:T(8,128)(2,1)}, u32[]{:S(2)}, u32[]{:S(2)}) async-start(bf16[14,32,2048]{2,0,1:T(8,128)(2,1)} %copy.50), calls=%async_computation.1 | async-start | bytes 4194304 | tf_op jit(solution)/shard_map/all_to_all | solution.py:44
  293.7 3.0 multiply_convert_fusion.1
  296.7 2.4 copy.55
  299.1 23.0 %all-to-all-done.1 = bf16[14,32,2048]{2,0,1:T(8,128)(2,1)} async-done(((bf16[14,32,2048]{2,0,1:T(8,128)(2,1)}), bf16[14,32,2048]{2,0,1:T(8,128)(2,1)}, u32[]{:S(2)}, u32[]{:S(2)}) %all-to-all-start.1) | async-done | bytes 1835040 | tf_op jit(solution)/shard_map/all_to_all | solution.py:44
  322.1 4.5 %all-to-all-start.2 = ((bf16[14,32,2048]{2,0,1:T(8,128)(2,1)}), bf16[14,32,2048]{2,0,1:T(8,128)(2,1)S(1)}, u32[]{:S(2)}, u32[]{:S(2)}) async-start(bf16[14,32,2048]{2,0,1:T(8,128)(2,1)} %copy.55), calls=%async_computation.2 | async-start | bytes 4194304 | tf_op jit(solution)/shard_map/all_to_all | solution.py:44
  326.5 2.8 multiply_convert_fusion
  329.3 2.3 copy.60
  331.7 23.3 %all-to-all-done.2 = bf16[14,32,2048]{2,0,1:T(8,128)(2,1)S(1)} async-done(((bf16[14,32,2048]{2,0,1:T(8,128)(2,1)}), bf16[14,32,2048]{2,0,1:T(8,128)(2,1)S(1)}, u32[]{:S(2)}, u32[]{:S(2)}) %all-to-all-start.2) | async-done | bytes 1835040 | tf_op jit(solution)/shard_map/all_to_all | solution.py:44
  355.0 1.4 copy-done.4
  356.4 5.2 %all-to-all-start.3 = ((bf16[14,32,2048]{2,0,1:T(8,128)(2,1)}), bf16[14,32,2048]{2,0,1:T(8,128)(2,1)}, u32[]{:S(2)}, u32[]{:S(2)}) async-start(bf16[14,32,2048]{2,0,1:T(8,128)(2,1)} %copy.60), calls=%async_computation.3 | async-start | bytes 4194304 | tf_op jit(solution)/shard_map/all_to_all | solution.py:44
  363.1 3.9 fusion.4
  367.9 22.1 %all-to-all-done.3 = bf16[14,32,2048]{2,0,1:T(8,128)(2,1)} async-done(((bf16[14,32,2048]{2,0,1:T(8,128)(2,1)}), bf16[14,32,2048]{2,0,1:T(8,128)(2,1)}, u32[]{:S(2)}, u32[]{:S(2)}) %all-to-all-start.3) | async-done | bytes 1835040 | tf_op jit(solution)/shard_map/all_to_all | solution.py:44
  390.2 3.8 fusion.5
  394.2 3.8 fusion.6
  399.2 0.8 copy-done
  (53 shorter events, 4.5 us)
Async XLA Ops:
  7.2 1.4 copy-start.6
  7.2 2.5 copy-start.8
  13.2 11.5 %copy-start.7 = (bf16[24,2048]{1,0:T(8,128)(2,1)S(1)}, bf16[24,2048]{1,0:T(8,128)(2,1)}, u32[]{:S(2)}) copy-start(bf16[24,2048]{1,0:T(8,128)(2,1)} %param.18) | copy-start | bytes 294916
  13.2 88.8 %all-to-all-start = ((bf16[3,14,32,2048]{3,1,0,2:T(8,128)(2,1)}), bf16[3,14,32,2048]{3,1,0,2:T(8,128)(2,1)}, u32[]{:S(2)}, u32[]{:S(2)}) async-start(bf16[3,14,32,2048]{3,1,0,2:T(8,128)(2,1)} %bitcast.62), calls=%async_computation | async-start | bytes 12582912 | tf_op jit(solution)/shard_map/all_to_all | solution.py:21
  24.7 86.9 %all-gather.2.cloned.1.call-start = ((), (), s32[]{:S(2)}) async-start(), calls=%async_computation.4 | async-start | bytes 1671168 | tf_op jit(solution)/shard_map/all_gather | solution.py:28
  25.6 243.8 %all-reduce.2.cloned.1.call-start = ((), (), s32[]{:S(2)}) async-start(), calls=%async_computation.5 | async-start | bytes 6291456 | tf_op jit(solution)/shard_map/psum | solution.py:39
  111.6 3.3 copy-start.5
  111.6 3.3 copy-start.10
  114.8 2.0 copy-start.12
  269.4 3.7 copy-start.11
  269.4 3.7 copy-start.13
  269.4 3.7 copy-start.14
  276.7 16.9 %copy-start.1 = (bf16[384,2048]{1,0:T(8,128)(2,1)S(1)}, bf16[384,2048]{1,0:T(8,128)(2,1)}, u32[]{:S(2)}) copy-start(bf16[384,2048]{1,0:T(8,128)(2,1)} %param.19) | copy-start | bytes 4718596
  276.7 45.3 %all-to-all-start.1 = ((bf16[14,32,2048]{2,0,1:T(8,128)(2,1)}), bf16[14,32,2048]{2,0,1:T(8,128)(2,1)}, u32[]{:S(2)}, u32[]{:S(2)}) async-start(bf16[14,32,2048]{2,0,1:T(8,128)(2,1)} %copy.50), calls=%async_computation.1 | async-start | bytes 4194304 | tf_op jit(solution)/shard_map/all_to_all | solution.py:44
  322.1 32.9 %all-to-all-start.2 = ((bf16[14,32,2048]{2,0,1:T(8,128)(2,1)}), bf16[14,32,2048]{2,0,1:T(8,128)(2,1)S(1)}, u32[]{:S(2)}, u32[]{:S(2)}) async-start(bf16[14,32,2048]{2,0,1:T(8,128)(2,1)} %copy.55), calls=%async_computation.2 | async-start | bytes 4194304 | tf_op jit(solution)/shard_map/all_to_all | solution.py:44
  331.7 30.1 %copy-start.9 = (s32[32]{0:T(128)S(1)}, s32[32]{0:T(128)}, u32[]{:S(2)}) copy-start(s32[32]{0:T(128)} %param.22) | copy-start | bytes 388
  355.0 1.4 copy-start.4
  356.4 33.7 %all-to-all-start.3 = ((bf16[14,32,2048]{2,0,1:T(8,128)(2,1)}), bf16[14,32,2048]{2,0,1:T(8,128)(2,1)}, u32[]{:S(2)}, u32[]{:S(2)}) async-start(bf16[14,32,2048]{2,0,1:T(8,128)(2,1)} %copy.60), calls=%async_computation.3 | async-start | bytes 4194304 | tf_op jit(solution)/shard_map/all_to_all | solution.py:44
  361.5 1.0 slice-start
  363.1 3.9 copy-start.2
  398.2 1.0 copy-start.3
  399.2 0.8 copy-start
Sparse Core Ops, SparseCore 0:
  28.1 64.7 all-gather.1
  119.7 149.6 all-reduce.1
